TPU v7x, 256 devices: a whole 4x4x8 slice. The times are simulated.
256 devices in a mesh: cx: 16 (over x, y), cy: 16 (over z, core).
Axes of the slice: x: 4, y: 4, z: 8, core: 2. Of those that a mesh axis runs over, the one named last changes fastest.
Arguments:
- query_rows: bfloat16 [65536, 1024], P(('cx', 'cy')), may hold values from -6 to 6
- key_rows: bfloat16 [65536, 1024], P(('cx', 'cy')), may hold values from -6 to 6
- value_rows: bfloat16 [65536, 1024], P(('cx', 'cy')), may hold values from -6 to 6
- forward_out: bfloat16 [65536, 1024], P(('cx', 'cy')), may hold values from -6 to 6
- out_grad: bfloat16 [65536, 1024], P(('cx', 'cy')), may hold values from -6 to 6
- doc_blocks: int32 [64], replicated, may hold values from 1 to 15, 512 in all
Outputs:
- query_grad: bfloat16 [65536, 1024], P(('cx', 'cy'))
- key_grad: bfloat16 [65536, 1024], P(('cx', 'cy'))
- value_grad: bfloat16 [65536, 1024], P(('cx', 'cy'))
Inputs may be any that keep to these rules, and one draw needn't show every extreme that they name: `doc_blocks`: lengths of the documents in blocks of 128 tokens, in sequence order, summing to 512; the longest has exactly 15 blocks.
All inputs are finite; a program needn't handle non-finite values.
Results may differ from a plain program's by a relative error of at most 0.0049.
Values may be sent and summed in bfloat16 or wider, within the bound.
No kernel may reach another device: no remote copies, remote signals or barrier semaphores. Data moves between devices by JAX's collectives and lax.ppermute only.
A program may use at most 128 MiB of HBM per device.

v0:
```python
import math

import jax
import jax.numpy as jnp
from jax import lax
from jax.sharding import PartitionSpec as P

HEADS = 8
DH = 128
BLOCK = 128
REACH = 7
GROUPS = 1


def from_behind(value, axis, steps):
    count = lax.axis_size(axis)
    first, last = (max(0, -steps), min(count, count - steps))
    return lax.ppermute(value, axis, [(source, source + steps) for source in range(first, last)])


def doc_window(doc_blocks, first_block, count):
    ends = jnp.cumsum(doc_blocks)
    starts = ends - doc_blocks
    block_ids = first_block + jnp.arange(count, dtype=jnp.int32)
    found = jnp.sum((starts[None, :] <= block_ids[:, None]).astype(jnp.int32), axis=1) - 1
    return jnp.where(block_ids >= ends[-1], -2, found)


def per_device(query_rows, key_rows, value_rows, forward_out, out_grad, doc_blocks):
    rows, features = query_rows.shape
    scale = 1.0 / math.sqrt(DH)
    axes = ("cx", "cy")
    shard = lax.axis_index(axes)
    per_shard = rows // BLOCK
    window = REACH + 1
    block_docs = doc_window(doc_blocks, shard * per_shard, window * per_shard)
    token_docs = jnp.repeat(block_docs, BLOCK)
    key_docs = token_docs[:rows]
    offsets = jnp.arange(rows, dtype=jnp.int32)

    def allowed(step):
        query_docs = token_docs[step * rows : (step + 1) * rows]
        mask = query_docs[:, None] == key_docs[None, :]
        if step == 0:
            mask = mask & (offsets[None, :] <= offsets[:, None])
        return mask

    masks = [allowed(step) for step in range(window)]

    def to_heads(x):
        return x.reshape(rows, HEADS, DH).transpose(1, 0, 2)

    def from_heads(x):
        return x.transpose(1, 0, 2).reshape(rows, features)

    query_h = to_heads(query_rows)
    grad_h = to_heads(out_grad)
    key_h = to_heads(key_rows)
    value_h = to_heads(value_rows)
    delta = jnp.einsum(
        "hqd,hqd->hq", grad_h, to_heads(forward_out), preferred_element_type=jnp.float32
    )

    def scores_of(q, k, mask):
        s = jnp.einsum("hqd,hkd->hqk", q, k, preferred_element_type=jnp.float32) * scale
        return jnp.where(mask[None], s, -1e30)

    group = HEADS // GROUPS
    query_grads, key_grads, value_grads = [], [], []
    for g in range(GROUPS):
        heads = slice(g * group, (g + 1) * group)
        q_own, do_own, k_own, v_own = query_h[heads], grad_h[heads], key_h[heads], value_h[heads]
        delta_own = delta[heads]

        scores = scores_of(q_own, k_own, masks[0])
        top = jnp.max(scores, axis=2)
        total = jnp.sum(jnp.exp(scores - top[..., None]), axis=2)
        stored = [(q_own, do_own, delta_own)]
        stats = [(top, total)]
        big = jnp.stack([q_own, do_own])
        small = jnp.concatenate([top, total, delta_own], axis=1)
        for step in range(1, window):
            big = from_behind(big, axes, -1)
            small = from_behind(small, axes, -1)
            q_in, do_in = big[0], big[1]
            top_in, total_in, delta_in = small[:, :rows], small[:, rows : 2 * rows], small[:, 2 * rows :]
            scores = scores_of(q_in, k_own, masks[step])
            part_top = jnp.max(scores, axis=2)
            part_total = jnp.sum(jnp.exp(scores - part_top[..., None]), axis=2)
            merged_top = jnp.maximum(top_in, part_top)
            merged_total = total_in * jnp.exp(top_in - merged_top) + part_total * jnp.exp(
                part_top - merged_top
            )
            stored.append((q_in, do_in, delta_in))
            stats.append((merged_top, merged_total))
            if step < window - 1:
                small = jnp.concatenate([merged_top, merged_total, delta_in], axis=1)

        key_acc = None
        value_acc = None
        carry = None
        for stage in range(window):
            step = window - 1 - stage
            q_in, do_in, delta_in = stored[step]
            local_lse = stats[step][0] + jnp.log(stats[step][1])
            if stage == 0:
                lse = local_lse
                dq_in = None
            else:
                dq_in, lse_in = from_behind(carry, axes, 1)
                lse = jnp.where(shard == 0, local_lse, lse_in)
            mask = masks[step]
            scores = scores_of(q_in, k_own, mask)
            prob = jnp.where(mask[None], jnp.exp(scores - lse[..., None]), 0.0)
            dprob = jnp.einsum("hqd,hkd->hqk", do_in, v_own, preferred_element_type=jnp.float32)
            dscore = (prob * (dprob - delta_in[..., None])).astype(jnp.bfloat16)
            dq_part = jnp.einsum("hqk,hkd->hqd", dscore, k_own, preferred_element_type=jnp.float32)
            key_part = jnp.einsum("hqk,hqd->hkd", dscore, q_in, preferred_element_type=jnp.float32)
            value_part = jnp.einsum(
                "hqk,hqd->hkd", prob.astype(jnp.bfloat16), do_in, preferred_element_type=jnp.float32
            )
            key_acc = key_part if key_acc is None else key_acc + key_part
            value_acc = value_part if value_acc is None else value_acc + value_part
            dq_out = dq_part if dq_in is None else dq_in + dq_part
            if stage < window - 1:
                carry = (dq_out, lse)
        query_grads.append(dq_out)
        key_grads.append(key_acc)
        value_grads.append(value_acc)
    query_grad = from_heads(jnp.concatenate(query_grads) * scale).astype(jnp.bfloat16)
    key_grad = from_heads(jnp.concatenate(key_grads) * scale).astype(jnp.bfloat16)
    value_grad = from_heads(jnp.concatenate(value_grads)).astype(jnp.bfloat16)
    return (query_grad, key_grad, value_grad)


def solution(mesh):
    in_specs = (
        P(("cx", "cy"), None),
        P(("cx", "cy"), None),
        P(("cx", "cy"), None),
        P(("cx", "cy"), None),
        P(("cx", "cy"), None),
        P(),
    )
    out_specs = (P(("cx", "cy"), None), P(("cx", "cy"), None), P(("cx", "cy"), None))
    return jax.shard_map(
        per_device, mesh=mesh, in_specs=in_specs, out_specs=out_specs, check_vma=False
    )
```

profile of v0, /device:TPU:6, one launch (start us, length us, event | category | flops | bytes accessed | tf_op | source)
XLA Modules:
  0.0 324.7 jit_solution(13779622551656312551)
XLA Ops:
  4.0 9.9 %collective-permute-start = (bf16[2,8,256,128]{3,2,1,0:T(8,128)(2,1)}, bf16[2,8,256,128]{3,2,1,0:T(8,128)(2,1)}, u32[]{:S(2)}, u32[]{:S(2)}) collective-permute-start(bf16[2,8,256,128]{3,2,1,0:T(8,128)(2,1)} %pad_maximum_fusion), channel_id=1, source_target_pairs={{1,0},{2,1},{3,2},{4,3},{5,4},{6,5},{7,6},{8,7},{9,8},{10,9},{11,1... | collective-permute-start | bytes 3145736 | tf_op jit(solution)/shard_map/ppermute | solution.py:18
  18.5 8.0 %collective-permute-done = bf16[2,8,256,128]{3,2,1,0:T(8,128)(2,1)} collective-permute-done((bf16[2,8,256,128]{3,2,1,0:T(8,128)(2,1)}, bf16[2,8,256,128]{3,2,1,0:T(8,128)(2,1)}, u32[]{:S(2)}, u32[]{:S(2)}) %collective-permute-start) | collective-permute-done | bytes 1048608 | tf_op jit(solution)/shard_map/ppermute | solution.py:18
  26.5 8.0 %collective-permute-start.1 = (bf16[2,8,256,128]{3,2,1,0:T(8,128)(2,1)}, bf16[2,8,256,128]{3,2,1,0:T(8,128)(2,1)}, u32[]{:S(2)}, u32[]{:S(2)}) collective-permute-start(bf16[2,8,256,128]{3,2,1,0:T(8,128)(2,1)} %collective-permute-done), channel_id=1, source_target_pairs={{1,0},{2,1},{3,2},{4,3},{5,4},{6,5},{7,6},{8,7},{9,8},{10,9},{11,1... | collective-permute-start | bytes 3145736 | tf_op jit(solution)/shard_map/ppermute | solution.py:18
  35.9 11.3 %collective-permute-done.1 = bf16[2,8,256,128]{3,2,1,0:T(8,128)(2,1)} collective-permute-done((bf16[2,8,256,128]{3,2,1,0:T(8,128)(2,1)}, bf16[2,8,256,128]{3,2,1,0:T(8,128)(2,1)}, u32[]{:S(2)}, u32[]{:S(2)}) %collective-permute-start.1) | collective-permute-done | bytes 1048608 | tf_op jit(solution)/shard_map/ppermute | solution.py:18
  47.2 8.0 %collective-permute-start.2 = (bf16[2,8,256,128]{3,2,1,0:T(8,128)(2,1)}, bf16[2,8,256,128]{3,2,1,0:T(8,128)(2,1)}, u32[]{:S(2)}, u32[]{:S(2)}) collective-permute-start(bf16[2,8,256,128]{3,2,1,0:T(8,128)(2,1)} %collective-permute-done.1), channel_id=1, source_target_pairs={{1,0},{2,1},{3,2},{4,3},{5,4},{6,5},{7,6},{8,7},{9,8},{10,9},{11,1... | collective-permute-start | bytes 3145736 | tf_op jit(solution)/shard_map/ppermute | solution.py:18
  61.6 6.3 %collective-permute-done.2 = bf16[2,8,256,128]{3,2,1,0:T(8,128)(2,1)} collective-permute-done((bf16[2,8,256,128]{3,2,1,0:T(8,128)(2,1)}, bf16[2,8,256,128]{3,2,1,0:T(8,128)(2,1)}, u32[]{:S(2)}, u32[]{:S(2)}) %collective-permute-start.2) | collective-permute-done | bytes 1048608 | tf_op jit(solution)/shard_map/ppermute | solution.py:18
  67.8 8.0 %collective-permute-start.3 = (bf16[2,8,256,128]{3,2,1,0:T(8,128)(2,1)}, bf16[2,8,256,128]{3,2,1,0:T(8,128)(2,1)S(1)}, u32[]{:S(2)}, u32[]{:S(2)}) collective-permute-start(bf16[2,8,256,128]{3,2,1,0:T(8,128)(2,1)} %collective-permute-done.2), channel_id=1, source_target_pairs={{1,0},{2,1},{3,2},{4,3},{5,4},{6,5},{7,6},{8,7},{9,8},{10,9},{11,1... | collective-permute-start | bytes 3145736 | tf_op jit(solution)/shard_map/ppermute | solution.py:18
  80.4 8.2 %collective-permute-done.8 = f32[8,768]{1,0:T(8,128)S(1)} collective-permute-done((f32[8,768]{1,0:T(8,128)S(1)}, f32[8,768]{1,0:T(8,128)S(1)}, u32[]{:S(2)}, u32[]{:S(2)}) %collective-permute-start.8) | collective-permute-done | bytes 24608 | tf_op jit(solution)/shard_map/ppermute | solution.py:18
  88.7 8.0 %collective-permute-start.9 = (f32[8,768]{1,0:T(8,128)S(1)}, f32[8,768]{1,0:T(8,128)S(1)}, u32[]{:S(2)}, u32[]{:S(2)}) collective-permute-start(f32[8,768]{1,0:T(8,128)S(1)} %pad_maximum_fusion.3), channel_id=1, source_target_pairs={{1,0},{2,1},{3,2},{4,3},{5,4},{6,5},{7,6},{8,7},{9,8},{10,9},{11,1... | collective-permute-start | bytes 73736 | tf_op jit(solution)/shard_map/ppermute | solution.py:18
  100.6 5.5 %collective-permute-start.10 = (f32[8,768]{1,0:T(8,128)S(1)}, f32[8,768]{1,0:T(8,128)S(1)}, u32[]{:S(2)}, u32[]{:S(2)}) collective-permute-start(f32[8,768]{1,0:T(8,128)S(1)} %pad_maximum_fusion.4), channel_id=1, source_target_pairs={{1,0},{2,1},{3,2},{4,3},{5,4},{6,5},{7,6},{8,7},{9,8},{10,9},{11,1... | collective-permute-start | bytes 73736 | tf_op jit(solution)/shard_map/ppermute | solution.py:18
  106.7 4.3 %collective-permute-done.4 = bf16[2,8,256,128]{3,2,1,0:T(8,128)(2,1)S(1)} collective-permute-done((bf16[2,8,256,128]{3,2,1,0:T(8,128)(2,1)S(1)}, bf16[2,8,256,128]{3,2,1,0:T(8,128)(2,1)S(1)}, u32[]{:S(2)}, u32[]{:S(2)}) %collective-permute-start.4) | collective-permute-done | bytes 1048608 | tf_op jit(solution)/shard_map/ppermute | solution.py:18
  110.9 8.0 %collective-permute-start.5 = (bf16[2,8,256,128]{3,2,1,0:T(8,128)(2,1)S(1)}, bf16[2,8,256,128]{3,2,1,0:T(8,128)(2,1)S(1)}, u32[]{:S(2)}, u32[]{:S(2)}) collective-permute-start(bf16[2,8,256,128]{3,2,1,0:T(8,128)(2,1)S(1)} %collective-permute-done.4), channel_id=1, source_target_pairs={{1,0},{2,1},{3,2},{4,3},{5,4},{6,5},{7,6},{8,7},{9,8},{10,9},{11,1... | collective-permute-start | bytes 3145736 | tf_op jit(solution)/shard_map/ppermute | solution.py:18
  122.1 9.1 %collective-permute-done.5 = bf16[2,8,256,128]{3,2,1,0:T(8,128)(2,1)S(1)} collective-permute-done((bf16[2,8,256,128]{3,2,1,0:T(8,128)(2,1)S(1)}, bf16[2,8,256,128]{3,2,1,0:T(8,128)(2,1)S(1)}, u32[]{:S(2)}, u32[]{:S(2)}) %collective-permute-start.5) | collective-permute-done | bytes 1048608 | tf_op jit(solution)/shard_map/ppermute | solution.py:18
  131.3 8.0 %collective-permute-start.6 = (bf16[2,8,256,128]{3,2,1,0:T(8,128)(2,1)S(1)}, bf16[2,8,256,128]{3,2,1,0:T(8,128)(2,1)S(1)}, u32[]{:S(2)}, u32[]{:S(2)}) collective-permute-start(bf16[2,8,256,128]{3,2,1,0:T(8,128)(2,1)S(1)} %collective-permute-done.5), channel_id=1, source_target_pairs={{1,0},{2,1},{3,2},{4,3},{5,4},{6,5},{7,6},{8,7},{9,8},{10,9},{11,1... | collective-permute-start | bytes 3145736 | tf_op jit(solution)/shard_map/ppermute | solution.py:18
  142.1 9.7 %collective-permute-done.12 = f32[8,768]{1,0:T(8,128)S(1)} collective-permute-done((f32[8,768]{1,0:T(8,128)S(1)}, f32[8,768]{1,0:T(8,128)S(1)}, u32[]{:S(2)}, u32[]{:S(2)}) %collective-permute-start.12) | collective-permute-done | bytes 24608 | tf_op jit(solution)/shard_map/ppermute | solution.py:18
  151.9 8.0 %collective-permute-start.13 = (f32[8,768]{1,0:T(8,128)S(1)}, f32[8,768]{1,0:T(8,128)S(1)}, u32[]{:S(2)}, u32[]{:S(2)}) collective-permute-start(f32[8,768]{1,0:T(8,128)S(1)} %pad_maximum_fusion.7), channel_id=1, source_target_pairs={{1,0},{2,1},{3,2},{4,3},{5,4},{6,5},{7,6},{8,7},{9,8},{10,9},{11,1... | collective-permute-start | bytes 73736 | tf_op jit(solution)/shard_map/ppermute | solution.py:18
  175.2 9.9 %collective-permute-done.17 = f32[8,256]{1,0:T(8,128)S(1)} collective-permute-done((f32[8,256]{1,0:T(8,128)S(1)}, f32[8,256]{1,0:T(8,128)S(1)}, u32[]{:S(2)}, u32[]{:S(2)}) %collective-permute-start.17) | collective-permute-done | bytes 8224 | tf_op jit(solution)/shard_map/ppermute | solution.py:18
  190.3 4.1 %collective-permute-done.19 = f32[8,256]{1,0:T(8,128)S(1)} collective-permute-done((f32[8,256]{1,0:T(8,128)S(1)}, f32[8,256]{1,0:T(8,128)S(1)}, u32[]{:S(2)}, u32[]{:S(2)}) %collective-permute-start.19) | collective-permute-done | bytes 8224 | tf_op jit(solution)/shard_map/ppermute | solution.py:18
  207.2 11.2 %collective-permute-done.16 = f32[8,256,128]{2,1,0:T(8,128)S(1)} collective-permute-done((f32[8,256,128]{2,1,0:T(8,128)S(1)}, f32[8,256,128]{2,1,0:T(8,128)S(1)}, u32[]{:S(2)}, u32[]{:S(2)}) %collective-permute-start.16) | collective-permute-done | bytes 1048608 | tf_op jit(solution)/shard_map/ppermute | solution.py:18
  226.9 11.9 %collective-permute-done.18 = f32[8,256,128]{2,1,0:T(8,128)S(1)} collective-permute-done((f32[8,256,128]{2,1,0:T(8,128)S(1)}, f32[8,256,128]{2,1,0:T(8,128)S(1)}, u32[]{:S(2)}, u32[]{:S(2)}) %collective-permute-start.18) | collective-permute-done | bytes 1048608 | tf_op jit(solution)/shard_map/ppermute | solution.py:18
  247.4 11.9 %collective-permute-done.20 = f32[8,256,128]{2,1,0:T(8,128)S(1)} collective-permute-done((f32[8,256,128]{2,1,0:T(8,128)S(1)}, f32[8,256,128]{2,1,0:T(8,128)S(1)}, u32[]{:S(2)}, u32[]{:S(2)}) %collective-permute-start.20) | collective-permute-done | bytes 1048608 | tf_op jit(solution)/shard_map/ppermute | solution.py:18
  267.2 12.6 %collective-permute-done.22 = f32[8,256,128]{2,1,0:T(8,128)S(1)} collective-permute-done((f32[8,256,128]{2,1,0:T(8,128)S(1)}, f32[8,256,128]{2,1,0:T(8,128)S(1)}, u32[]{:S(2)}, u32[]{:S(2)}) %collective-permute-start.22) | collective-permute-done | bytes 1048608 | tf_op jit(solution)/shard_map/ppermute | solution.py:18
  286.7 13.7 %collective-permute-done.24 = f32[8,256,128]{2,1,0:T(8,128)S(1)} collective-permute-done((f32[8,256,128]{2,1,0:T(8,128)S(1)}, f32[8,256,128]{2,1,0:T(8,128)S(1)}, u32[]{:S(2)}, u32[]{:S(2)}) %collective-permute-start.24) | collective-permute-done | bytes 1048608 | tf_op jit(solution)/shard_map/ppermute | solution.py:18
  315.7 6.4 %collective-permute-done.26 = f32[8,256,128]{2,1,0:T(8,128)} collective-permute-done((f32[8,256,128]{2,1,0:T(8,128)}, f32[8,256,128]{2,1,0:T(8,128)}, u32[]{:S(2)}, u32[]{:S(2)}) %collective-permute-start.26) | collective-permute-done | bytes 1048608 | tf_op jit(solution)/shard_map/ppermute | solution.py:18
  (176 shorter events, 112.9 us)
Async XLA Ops:
  4.0 22.5 %collective-permute-start = (bf16[2,8,256,128]{3,2,1,0:T(8,128)(2,1)}, bf16[2,8,256,128]{3,2,1,0:T(8,128)(2,1)}, u32[]{:S(2)}, u32[]{:S(2)}) collective-permute-start(bf16[2,8,256,128]{3,2,1,0:T(8,128)(2,1)} %pad_maximum_fusion), channel_id=1, source_target_pairs={{1,0},{2,1},{3,2},{4,3},{5,4},{6,5},{7,6},{8,7},{9,8},{10,9},{11,1... | collective-permute-start | bytes 3145736 | tf_op jit(solution)/shard_map/ppermute | solution.py:18
  26.5 20.6 %collective-permute-start.1 = (bf16[2,8,256,128]{3,2,1,0:T(8,128)(2,1)}, bf16[2,8,256,128]{3,2,1,0:T(8,128)(2,1)}, u32[]{:S(2)}, u32[]{:S(2)}) collective-permute-start(bf16[2,8,256,128]{3,2,1,0:T(8,128)(2,1)} %collective-permute-done), channel_id=1, source_target_pairs={{1,0},{2,1},{3,2},{4,3},{5,4},{6,5},{7,6},{8,7},{9,8},{10,9},{11,1... | collective-permute-start | bytes 3145736 | tf_op jit(solution)/shard_map/ppermute | solution.py:18
  47.2 20.6 %collective-permute-start.2 = (bf16[2,8,256,128]{3,2,1,0:T(8,128)(2,1)}, bf16[2,8,256,128]{3,2,1,0:T(8,128)(2,1)}, u32[]{:S(2)}, u32[]{:S(2)}) collective-permute-start(bf16[2,8,256,128]{3,2,1,0:T(8,128)(2,1)} %collective-permute-done.1), channel_id=1, source_target_pairs={{1,0},{2,1},{3,2},{4,3},{5,4},{6,5},{7,6},{8,7},{9,8},{10,9},{11,1... | collective-permute-start | bytes 3145736 | tf_op jit(solution)/shard_map/ppermute | solution.py:18
  57.8 18.1 %collective-permute-start.7 = (f32[8,768]{1,0:T(8,128)}, f32[8,768]{1,0:T(8,128)}, u32[]{:S(2)}, u32[]{:S(2)}) collective-permute-start(f32[8,768]{1,0:T(8,128)} %pad_maximum_fusion.1), channel_id=1, source_target_pairs={{1,0},{2,1},{3,2},{4,3},{5,4},{6,5},{7,6},{8,7},{9,8},{10,9},{11,1... | collective-permute-start | bytes 73736 | tf_op jit(solution)/shard_map/ppermute | solution.py:18
  67.8 28.9 %collective-permute-start.3 = (bf16[2,8,256,128]{3,2,1,0:T(8,128)(2,1)}, bf16[2,8,256,128]{3,2,1,0:T(8,128)(2,1)S(1)}, u32[]{:S(2)}, u32[]{:S(2)}) collective-permute-start(bf16[2,8,256,128]{3,2,1,0:T(8,128)(2,1)} %collective-permute-done.2), channel_id=1, source_target_pairs={{1,0},{2,1},{3,2},{4,3},{5,4},{6,5},{7,6},{8,7},{9,8},{10,9},{11,1... | collective-permute-start | bytes 3145736 | tf_op jit(solution)/shard_map/ppermute | solution.py:18
  76.6 12.0 %collective-permute-start.8 = (f32[8,768]{1,0:T(8,128)S(1)}, f32[8,768]{1,0:T(8,128)S(1)}, u32[]{:S(2)}, u32[]{:S(2)}) collective-permute-start(f32[8,768]{1,0:T(8,128)S(1)} %pad_maximum_fusion.2), channel_id=1, source_target_pairs={{1,0},{2,1},{3,2},{4,3},{5,4},{6,5},{7,6},{8,7},{9,8},{10,9},{11,1... | collective-permute-start | bytes 73736 | tf_op jit(solution)/shard_map/ppermute | solution.py:18
  88.7 11.9 %collective-permute-start.9 = (f32[8,768]{1,0:T(8,128)S(1)}, f32[8,768]{1,0:T(8,128)S(1)}, u32[]{:S(2)}, u32[]{:S(2)}) collective-permute-start(f32[8,768]{1,0:T(8,128)S(1)} %pad_maximum_fusion.3), channel_id=1, source_target_pairs={{1,0},{2,1},{3,2},{4,3},{5,4},{6,5},{7,6},{8,7},{9,8},{10,9},{11,1... | collective-permute-start | bytes 73736 | tf_op jit(solution)/shard_map/ppermute | solution.py:18
  96.7 14.2 %collective-permute-start.4 = (bf16[2,8,256,128]{3,2,1,0:T(8,128)(2,1)S(1)}, bf16[2,8,256,128]{3,2,1,0:T(8,128)(2,1)S(1)}, u32[]{:S(2)}, u32[]{:S(2)}) collective-permute-start(bf16[2,8,256,128]{3,2,1,0:T(8,128)(2,1)S(1)} %collective-permute-done.3), channel_id=1, source_target_pairs={{1,0},{2,1},{3,2},{4,3},{5,4},{6,5},{7,6},{8,7},{9,8},{10,9},{11,1... | collective-permute-start | bytes 3145736 | tf_op jit(solution)/shard_map/ppermute | solution.py:18
  100.6 18.7 %collective-permute-start.10 = (f32[8,768]{1,0:T(8,128)S(1)}, f32[8,768]{1,0:T(8,128)S(1)}, u32[]{:S(2)}, u32[]{:S(2)}) collective-permute-start(f32[8,768]{1,0:T(8,128)S(1)} %pad_maximum_fusion.4), channel_id=1, source_target_pairs={{1,0},{2,1},{3,2},{4,3},{5,4},{6,5},{7,6},{8,7},{9,8},{10,9},{11,1... | collective-permute-start | bytes 73736 | tf_op jit(solution)/shard_map/ppermute | solution.py:18
  110.9 20.3 %collective-permute-start.5 = (bf16[2,8,256,128]{3,2,1,0:T(8,128)(2,1)S(1)}, bf16[2,8,256,128]{3,2,1,0:T(8,128)(2,1)S(1)}, u32[]{:S(2)}, u32[]{:S(2)}) collective-permute-start(bf16[2,8,256,128]{3,2,1,0:T(8,128)(2,1)S(1)} %collective-permute-done.4), channel_id=1, source_target_pairs={{1,0},{2,1},{3,2},{4,3},{5,4},{6,5},{7,6},{8,7},{9,8},{10,9},{11,1... | collective-permute-start | bytes 3145736 | tf_op jit(solution)/shard_map/ppermute | solution.py:18
  119.3 20.0 %collective-permute-start.11 = (f32[8,768]{1,0:T(8,128)S(1)}, f32[8,768]{1,0:T(8,128)S(1)}, u32[]{:S(2)}, u32[]{:S(2)}) collective-permute-start(f32[8,768]{1,0:T(8,128)S(1)} %pad_maximum_fusion.5), channel_id=1, source_target_pairs={{1,0},{2,1},{3,2},{4,3},{5,4},{6,5},{7,6},{8,7},{9,8},{10,9},{11,1... | collective-permute-start | bytes 73736 | tf_op jit(solution)/shard_map/ppermute | solution.py:18
  131.3 28.7 %collective-permute-start.6 = (bf16[2,8,256,128]{3,2,1,0:T(8,128)(2,1)S(1)}, bf16[2,8,256,128]{3,2,1,0:T(8,128)(2,1)S(1)}, u32[]{:S(2)}, u32[]{:S(2)}) collective-permute-start(bf16[2,8,256,128]{3,2,1,0:T(8,128)(2,1)S(1)} %collective-permute-done.5), channel_id=1, source_target_pairs={{1,0},{2,1},{3,2},{4,3},{5,4},{6,5},{7,6},{8,7},{9,8},{10,9},{11,1... | collective-permute-start | bytes 3145736 | tf_op jit(solution)/shard_map/ppermute | solution.py:18
  139.3 12.5 %collective-permute-start.12 = (f32[8,768]{1,0:T(8,128)S(1)}, f32[8,768]{1,0:T(8,128)S(1)}, u32[]{:S(2)}, u32[]{:S(2)}) collective-permute-start(f32[8,768]{1,0:T(8,128)S(1)} %pad_maximum_fusion.6), channel_id=1, source_target_pairs={{1,0},{2,1},{3,2},{4,3},{5,4},{6,5},{7,6},{8,7},{9,8},{10,9},{11,1... | collective-permute-start | bytes 73736 | tf_op jit(solution)/shard_map/ppermute | solution.py:18
  164.7 32.8 %collective-permute-start.14 = (f32[8,256,128]{2,1,0:T(8,128)S(1)}, f32[8,256,128]{2,1,0:T(8,128)S(1)}, u32[]{:S(2)}, u32[]{:S(2)}) collective-permute-start(f32[8,256,128]{2,1,0:T(8,128)S(1)} %fusion.108), channel_id=1, source_target_pairs={{0,1},{1,2},{2,3},{3,4},{4,5},{5,6},{6,7},{7,8},{8,9},{9,10},{10,1... | collective-permute-start | bytes 3145736 | tf_op jit(solution)/shard_map/ppermute | solution.py:18
  170.6 14.5 %collective-permute-start.17 = (f32[8,256]{1,0:T(8,128)S(1)}, f32[8,256]{1,0:T(8,128)S(1)}, u32[]{:S(2)}, u32[]{:S(2)}) collective-permute-start(f32[8,256]{1,0:T(8,128)S(1)} %add_select_fusion.6), channel_id=1, source_target_pairs={{0,1},{1,2},{2,3},{3,4},{4,5},{5,6},{6,7},{7,8},{8,9},{9,10},{10,1... | collective-permute-start | bytes 24584 | tf_op jit(solution)/shard_map/ppermute | solution.py:18
  198.0 20.3 %collective-permute-start.16 = (f32[8,256,128]{2,1,0:T(8,128)S(1)}, f32[8,256,128]{2,1,0:T(8,128)S(1)}, u32[]{:S(2)}, u32[]{:S(2)}) collective-permute-start(f32[8,256,128]{2,1,0:T(8,128)S(1)} %convolution_add_fusion.2), channel_id=1, source_target_pairs={{0,1},{1,2},{2,3},{3,4},{4,5},{5,6},{6,7},{7,8},{8,9},{9,10},{10,1... | collective-permute-start | bytes 3145736 | tf_op jit(solution)/shard_map/ppermute | solution.py:18
  203.5 21.5 %collective-permute-start.23 = (f32[8,256]{1,0:T(8,128)S(1)}, f32[8,256]{1,0:T(8,128)S(1)}, u32[]{:S(2)}, u32[]{:S(2)}) collective-permute-start(f32[8,256]{1,0:T(8,128)S(1)} %add_select_fusion.3), channel_id=1, source_target_pairs={{0,1},{1,2},{2,3},{3,4},{4,5},{5,6},{6,7},{7,8},{8,9},{9,10},{10,1... | collective-permute-start | bytes 24584 | tf_op jit(solution)/shard_map/ppermute | solution.py:18
  218.5 20.3 %collective-permute-start.18 = (f32[8,256,128]{2,1,0:T(8,128)S(1)}, f32[8,256,128]{2,1,0:T(8,128)S(1)}, u32[]{:S(2)}, u32[]{:S(2)}) collective-permute-start(f32[8,256,128]{2,1,0:T(8,128)S(1)} %add.162), channel_id=1, source_target_pairs={{0,1},{1,2},{2,3},{3,4},{4,5},{5,6},{6,7},{7,8},{8,9},{9,10},{10,1... | collective-permute-start | bytes 3145736 | tf_op jit(solution)/shard_map/ppermute | solution.py:18
  225.0 36.4 %collective-permute-start.25 = (f32[8,256]{1,0:T(8,128)S(1)}, f32[8,256]{1,0:T(8,128)S(1)}, u32[]{:S(2)}, u32[]{:S(2)}) collective-permute-start(f32[8,256]{1,0:T(8,128)S(1)} %add_select_fusion.2), channel_id=1, source_target_pairs={{0,1},{1,2},{2,3},{3,4},{4,5},{5,6},{6,7},{7,8},{8,9},{9,10},{10,1... | collective-permute-start | bytes 24584 | tf_op jit(solution)/shard_map/ppermute | solution.py:18
  239.0 20.3 %collective-permute-start.20 = (f32[8,256,128]{2,1,0:T(8,128)S(1)}, f32[8,256,128]{2,1,0:T(8,128)S(1)}, u32[]{:S(2)}, u32[]{:S(2)}) collective-permute-start(f32[8,256,128]{2,1,0:T(8,128)S(1)} %add.164), channel_id=1, source_target_pairs={{0,1},{1,2},{2,3},{3,4},{4,5},{5,6},{6,7},{7,8},{8,9},{9,10},{10,1... | collective-permute-start | bytes 3145736 | tf_op jit(solution)/shard_map/ppermute | solution.py:18
  259.4 20.3 %collective-permute-start.22 = (f32[8,256,128]{2,1,0:T(8,128)S(1)}, f32[8,256,128]{2,1,0:T(8,128)S(1)}, u32[]{:S(2)}, u32[]{:S(2)}) collective-permute-start(f32[8,256,128]{2,1,0:T(8,128)S(1)} %add.166), channel_id=1, source_target_pairs={{0,1},{1,2},{2,3},{3,4},{4,5},{5,6},{6,7},{7,8},{8,9},{9,10},{10,1... | collective-permute-start | bytes 3145736 | tf_op jit(solution)/shard_map/ppermute | solution.py:18
  261.4 23.1 %collective-permute-start.27 = (f32[8,256]{1,0:T(8,128)S(1)}, f32[8,256]{1,0:T(8,128)S(1)}, u32[]{:S(2)}, u32[]{:S(2)}) collective-permute-start(f32[8,256]{1,0:T(8,128)S(1)} %add_select_fusion.1), channel_id=1, source_target_pairs={{0,1},{1,2},{2,3},{3,4},{4,5},{5,6},{6,7},{7,8},{8,9},{9,10},{10,1... | collective-permute-start | bytes 24584 | tf_op jit(solution)/shard_map/ppermute | solution.py:18
  279.9 20.5 %collective-permute-start.24 = (f32[8,256,128]{2,1,0:T(8,128)S(1)}, f32[8,256,128]{2,1,0:T(8,128)S(1)}, u32[]{:S(2)}, u32[]{:S(2)}) collective-permute-start(f32[8,256,128]{2,1,0:T(8,128)S(1)} %add.168), channel_id=1, source_target_pairs={{0,1},{1,2},{2,3},{3,4},{4,5},{5,6},{6,7},{7,8},{8,9},{9,10},{10,1... | collective-permute-start | bytes 3145736 | tf_op jit(solution)/shard_map/ppermute | solution.py:18
  301.4 20.6 %collective-permute-start.26 = (f32[8,256,128]{2,1,0:T(8,128)}, f32[8,256,128]{2,1,0:T(8,128)}, u32[]{:S(2)}, u32[]{:S(2)}) collective-permute-start(f32[8,256,128]{2,1,0:T(8,128)} %add.170), channel_id=1, source_target_pairs={{0,1},{1,2},{2,3},{3,4},{4,5},{5,6},{6,7},{7,8},{8,9},{9,10},{10,1... | collective-permute-start | bytes 3145736 | tf_op jit(solution)/shard_map/ppermute | solution.py:18
  (24 other events, 538.2 us)
where the time goes:
time: 326 us; the launch traced here: 325 us
  waiting for transfers between devices  145 us (44%)
  starting transfers between devices  109 us (33%)
  matrix products  47.9 us (15%)
  local copies, waits for them, and re-layouts  10.9 us (3%)
  other arithmetic  10.8 us (3%)
    ppermute x28, waiting for transfers between devices, from_behind(): lax.ppermute(value, axis, [(source, source + steps) for source in range(f...  145 us
    ppermute x28, starting transfers between devices, from_behind(): lax.ppermute(value, axis, [(source, source + steps) for source in range(f...  109 us
    dot_general x8, matrix products, per_device(): jnp.einsum('hqk,hqd->hkd', dscore, q_in, preferred_element_type=jnp.float32)  17.3 us
    dot_general x8, matrix products, per_device(): jnp.einsum('hqd,hkd->hqk', do_in, v_own, preferred_element_type=jnp.float32)  9.43 us
    dot_general x8, matrix products, per_device(): jnp.einsum('hqk,hqd->hkd', prob.astype(jnp.bfloat16), do_in, preferred_el...  8.71 us
    dot_general x8, matrix products, scores_of(): jnp.einsum('hqd,hkd->hqk', q, k, preferred_element_type=jnp.float32) * scale  8.56 us
    unnamed x46, local copies, waits for them, and re-layouts  6.96 us
  transfers between devices with their start and end apart: 28, of which 18 were waited for; matrix products, arithmetic and copies ran while one was open for 19% of the time, Pallas kernels for 0%

commit v1 on v0

--- a/solution.py
+++ b/solution.py
@@ -77,12 +77,12 @@
         total = jnp.sum(jnp.exp(scores - top[..., None]), axis=2)
         stored = [(q_own, do_own, delta_own)]
         stats = [(top, total)]
-        big = jnp.stack([q_own, do_own])
+        big = (q_own, do_own)
         small = jnp.concatenate([top, total, delta_own], axis=1)
         for step in range(1, window):
             big = from_behind(big, axes, -1)
             small = from_behind(small, axes, -1)
-            q_in, do_in = big[0], big[1]
+            q_in, do_in = big
             top_in, total_in, delta_in = small[:, :rows], small[:, rows : 2 * rows], small[:, 2 * rows :]
             scores = scores_of(q_in, k_own, masks[step])
             part_top = jnp.max(scores, axis=2)
@@ -107,7 +107,8 @@
                 lse = local_lse
                 dq_in = None
             else:
-                dq_in, lse_in = from_behind(carry, axes, 1)
+                dq_low, dq_high, lse_in = from_behind(carry, axes, 1)
+                dq_in = jnp.concatenate([dq_low, dq_high])
                 lse = jnp.where(shard == 0, local_lse, lse_in)
             mask = masks[step]
             scores = scores_of(q_in, k_own, mask)
@@ -123,7 +124,7 @@
             value_acc = value_part if value_acc is None else value_acc + value_part
             dq_out = dq_part if dq_in is None else dq_in + dq_part
             if stage < window - 1:
-                carry = (dq_out, lse)
+                carry = (dq_out[: group // 2], dq_out[group // 2 :], lse)
         query_grads.append(dq_out)
         key_grads.append(key_acc)
         value_grads.append(value_acc)

time: 326 us -> 305 us (0.936)
  waiting for transfers between devices: 145 us -> 105 us
  starting transfers between devices: 109 us -> 134 us
  matrix products: 47.9 us -> 40.9 us
    ppermute x28 -> x42, waiting for transfers between devices: 145 us -> 105 us  [from_behind(): lax.ppermute(value, axis, [(source, source + steps) for source in range(f...]
    ppermute x28 -> x42, starting transfers between devices: 109 us -> 134 us  [from_behind(): lax.ppermute(value, axis, [(source, source + steps) for source in range(f...]
    unnamed x46 -> x44, local copies, waits for them, and re-layouts: 6.96 us -> 6.25 us
  transfers between devices with their start and end apart: 28 -> 42, of which waited for: 18 -> 23; matrix products, arithmetic and copies ran while one was open for 19% -> 18% of each run, Pallas kernels for 0% -> 0%
where the time goes in v1:
time: 305 us; the launch traced here: 303 us
  starting transfers between devices  134 us (44%)
  waiting for transfers between devices  105 us (34%)
  matrix products  40.9 us (13%)
  local copies, waits for them, and re-layouts  13.1 us (4%)
  other arithmetic  7.74 us (3%)
    ppermute x42, starting transfers between devices, from_behind(): lax.ppermute(value, axis, [(source, source + steps) for source in range(f...  134 us
    ppermute x42, waiting for transfers between devices, from_behind(): lax.ppermute(value, axis, [(source, source + steps) for source in range(f...  105 us
    dot_general x8, matrix products, per_device(): jnp.einsum('hqk,hqd->hkd', dscore, q_in, preferred_element_type=jnp.float32)  15.2 us
    dot_general x8, matrix products, per_device(): jnp.einsum('hqd,hkd->hqk', do_in, v_own, preferred_element_type=jnp.float32)  7.4 us
    dot_general x8, matrix products, per_device(): jnp.einsum('hqk,hqd->hkd', prob.astype(jnp.bfloat16), do_in, preferred_el...  6.61 us
    dot_general x8, matrix products, scores_of(): jnp.einsum('hqd,hkd->hqk', q, k, preferred_element_type=jnp.float32) * scale  6.49 us
    unnamed x44, local copies, waits for them, and re-layouts  6.25 us
  transfers between devices with their start and end apart: 42, of which 23 were waited for; matrix products, arithmetic and copies ran while one was open for 18% of the time, Pallas kernels for 0%

profile of v1, /device:TPU:6, one launch (start us, length us, event | category | flops | bytes accessed | tf_op | source)
XLA Modules:
  0.0 303.1 jit_solution(8421699641478080219)
XLA Ops:
  3.0 10.0 %collective-permute-start.14 = (bf16[8,256,128]{2,1,0:T(8,128)(2,1)}, bf16[8,256,128]{2,1,0:T(8,128)(2,1)}, u32[]{:S(2)}, u32[]{:S(2)}) collective-permute-start(bf16[8,256,128]{2,1,0:T(8,128)(2,1)} %bitcast.10), channel_id=1, source_target_pairs={{1,0},{2,1},{3,2},{4,3},{5,4},{6,5},{7,6},{8,7},{9,8},{10,9},{11,1... | collective-permute-start | bytes 1572872 | tf_op jit(solution)/shard_map/ppermute | solution.py:18
  27.7 6.0 %collective-permute-start.1 = (bf16[8,256,128]{2,1,0:T(8,128)(2,1)}, bf16[8,256,128]{2,1,0:T(8,128)(2,1)S(1)}, u32[]{:S(2)}, u32[]{:S(2)}) collective-permute-start(bf16[8,256,128]{2,1,0:T(8,128)(2,1)} %collective-permute-done), channel_id=1, source_target_pairs={{1,0},{2,1},{3,2},{4,3},{5,4},{6,5},{7,6},{8,7},{9,8},{10,9},{11,1... | collective-permute-start | bytes 1572872 | tf_op jit(solution)/shard_map/ppermute | solution.py:18
  40.7 7.9 %collective-permute-start.2 = (bf16[8,256,128]{2,1,0:T(8,128)(2,1)S(1)}, bf16[8,256,128]{2,1,0:T(8,128)(2,1)S(1)}, u32[]{:S(2)}, u32[]{:S(2)}) collective-permute-start(bf16[8,256,128]{2,1,0:T(8,128)(2,1)S(1)} %collective-permute-done.1), channel_id=1, source_target_pairs={{1,0},{2,1},{3,2},{4,3},{5,4},{6,5},{7,6},{8,7},{9,8},{10,9},{11,1... | collective-permute-start | bytes 1572872 | tf_op jit(solution)/shard_map/ppermute | solution.py:18
  51.5 3.7 %collective-permute-start.16 = (bf16[8,256,128]{2,1,0:T(8,128)(2,1)S(1)}, bf16[8,256,128]{2,1,0:T(8,128)(2,1)S(1)}, u32[]{:S(2)}, u32[]{:S(2)}) collective-permute-start(bf16[8,256,128]{2,1,0:T(8,128)(2,1)S(1)} %collective-permute-done.15), channel_id=1, source_target_pairs={{1,0},{2,1},{3,2},{4,3},{5,4},{6,5},{7,6},{8,7},{9,8},{10,9},{11,1... | collective-permute-start | bytes 1572872 | tf_op jit(solution)/shard_map/ppermute | solution.py:18
  55.3 8.0 %collective-permute-start.3 = (bf16[8,256,128]{2,1,0:T(8,128)(2,1)S(1)}, bf16[8,256,128]{2,1,0:T(8,128)(2,1)S(1)}, u32[]{:S(2)}, u32[]{:S(2)}) collective-permute-start(bf16[8,256,128]{2,1,0:T(8,128)(2,1)S(1)} %collective-permute-done.2), channel_id=1, source_target_pairs={{1,0},{2,1},{3,2},{4,3},{5,4},{6,5},{7,6},{8,7},{9,8},{10,9},{11,1... | collective-permute-start | bytes 1572872 | tf_op jit(solution)/shard_map/ppermute | solution.py:18
  70.0 8.0 %collective-permute-start.4 = (bf16[8,256,128]{2,1,0:T(8,128)(2,1)S(1)}, bf16[8,256,128]{2,1,0:T(8,128)(2,1)S(1)}, u32[]{:S(2)}, u32[]{:S(2)}) collective-permute-start(bf16[8,256,128]{2,1,0:T(8,128)(2,1)S(1)} %collective-permute-done.3), channel_id=1, source_target_pairs={{1,0},{2,1},{3,2},{4,3},{5,4},{6,5},{7,6},{8,7},{9,8},{10,9},{11,1... | collective-permute-start | bytes 1572872 | tf_op jit(solution)/shard_map/ppermute | solution.py:18
  84.7 8.0 %collective-permute-start.5 = (bf16[8,256,128]{2,1,0:T(8,128)(2,1)S(1)}, bf16[8,256,128]{2,1,0:T(8,128)(2,1)S(1)}, u32[]{:S(2)}, u32[]{:S(2)}) collective-permute-start(bf16[8,256,128]{2,1,0:T(8,128)(2,1)S(1)} %collective-permute-done.4), channel_id=1, source_target_pairs={{1,0},{2,1},{3,2},{4,3},{5,4},{6,5},{7,6},{8,7},{9,8},{10,9},{11,1... | collective-permute-start | bytes 1572872 | tf_op jit(solution)/shard_map/ppermute | solution.py:18
  99.4 8.0 %collective-permute-start.6 = (bf16[8,256,128]{2,1,0:T(8,128)(2,1)S(1)}, bf16[8,256,128]{2,1,0:T(8,128)(2,1)S(1)}, u32[]{:S(2)}, u32[]{:S(2)}) collective-permute-start(bf16[8,256,128]{2,1,0:T(8,128)(2,1)S(1)} %collective-permute-done.5), channel_id=1, source_target_pairs={{1,0},{2,1},{3,2},{4,3},{5,4},{6,5},{7,6},{8,7},{9,8},{10,9},{11,1... | collective-permute-start | bytes 1572872 | tf_op jit(solution)/shard_map/ppermute | solution.py:18
  131.5 11.5 %collective-permute-done.26 = f32[8,256]{1,0:T(8,128)S(1)} collective-permute-done((f32[8,256]{1,0:T(8,128)S(1)}, f32[8,256]{1,0:T(8,128)S(1)}, u32[]{:S(2)}, u32[]{:S(2)}) %collective-permute-start.26) | collective-permute-done | bytes 8224 | tf_op jit(solution)/shard_map/ppermute | solution.py:18
  147.6 4.6 %collective-permute-done.29 = f32[8,256]{1,0:T(8,128)S(1)} collective-permute-done((f32[8,256]{1,0:T(8,128)S(1)}, f32[8,256]{1,0:T(8,128)S(1)}, u32[]{:S(2)}, u32[]{:S(2)}) %collective-permute-start.29) | collective-permute-done | bytes 8224 | tf_op jit(solution)/shard_map/ppermute | solution.py:18
  156.8 4.6 %collective-permute-done.32 = f32[8,256]{1,0:T(8,128)S(1)} collective-permute-done((f32[8,256]{1,0:T(8,128)S(1)}, f32[8,256]{1,0:T(8,128)S(1)}, u32[]{:S(2)}, u32[]{:S(2)}) %collective-permute-start.32) | collective-permute-done | bytes 8224 | tf_op jit(solution)/shard_map/ppermute | solution.py:18
  166.0 4.6 %collective-permute-done.35 = f32[8,256]{1,0:T(8,128)S(1)} collective-permute-done((f32[8,256]{1,0:T(8,128)S(1)}, f32[8,256]{1,0:T(8,128)S(1)}, u32[]{:S(2)}, u32[]{:S(2)}) %collective-permute-start.35) | collective-permute-done | bytes 8224 | tf_op jit(solution)/shard_map/ppermute | solution.py:18
  179.6 8.9 %collective-permute-done.24 = f32[4,256,128]{2,1,0:T(8,128)S(1)} collective-permute-done((f32[4,256,128]{2,1,0:T(8,128)S(1)}, f32[4,256,128]{2,1,0:T(8,128)S(1)}, u32[]{:S(2)}, u32[]{:S(2)}) %collective-permute-start.24) | collective-permute-done | bytes 524320 | tf_op jit(solution)/shard_map/ppermute | solution.py:18
  188.5 5.6 %collective-permute-done.25 = f32[4,256,128]{2,1,0:T(8,128)S(1)} collective-permute-done((f32[4,256,128]{2,1,0:T(8,128)S(1)}, f32[4,256,128]{2,1,0:T(8,128)S(1)}, u32[]{:S(2)}, u32[]{:S(2)}) %collective-permute-start.25) | collective-permute-done | bytes 524320 | tf_op jit(solution)/shard_map/ppermute | solution.py:18
  202.5 7.0 %collective-permute-done.27 = f32[4,256,128]{2,1,0:T(8,128)S(1)} collective-permute-done((f32[4,256,128]{2,1,0:T(8,128)S(1)}, f32[4,256,128]{2,1,0:T(8,128)S(1)}, u32[]{:S(2)}, u32[]{:S(2)}) %collective-permute-start.27) | collective-permute-done | bytes 524320 | tf_op jit(solution)/shard_map/ppermute | solution.py:18
  209.5 5.6 %collective-permute-done.28 = f32[4,256,128]{2,1,0:T(8,128)S(1)} collective-permute-done((f32[4,256,128]{2,1,0:T(8,128)S(1)}, f32[4,256,128]{2,1,0:T(8,128)S(1)}, u32[]{:S(2)}, u32[]{:S(2)}) %collective-permute-start.28) | collective-permute-done | bytes 524320 | tf_op jit(solution)/shard_map/ppermute | solution.py:18
  223.6 6.8 %collective-permute-done.30 = f32[4,256,128]{2,1,0:T(8,128)S(1)} collective-permute-done((f32[4,256,128]{2,1,0:T(8,128)S(1)}, f32[4,256,128]{2,1,0:T(8,128)S(1)}, u32[]{:S(2)}, u32[]{:S(2)}) %collective-permute-start.30) | collective-permute-done | bytes 524320 | tf_op jit(solution)/shard_map/ppermute | solution.py:18
  230.4 5.6 %collective-permute-done.31 = f32[4,256,128]{2,1,0:T(8,128)S(1)} collective-permute-done((f32[4,256,128]{2,1,0:T(8,128)S(1)}, f32[4,256,128]{2,1,0:T(8,128)S(1)}, u32[]{:S(2)}, u32[]{:S(2)}) %collective-permute-start.31) | collective-permute-done | bytes 524320 | tf_op jit(solution)/shard_map/ppermute | solution.py:18
  242.2 9.1 %collective-permute-done.33 = f32[4,256,128]{2,1,0:T(8,128)S(1)} collective-permute-done((f32[4,256,128]{2,1,0:T(8,128)S(1)}, f32[4,256,128]{2,1,0:T(8,128)S(1)}, u32[]{:S(2)}, u32[]{:S(2)}) %collective-permute-start.33) | collective-permute-done | bytes 524320 | tf_op jit(solution)/shard_map/ppermute | solution.py:18
  251.3 5.6 %collective-permute-done.34 = f32[4,256,128]{2,1,0:T(8,128)S(1)} collective-permute-done((f32[4,256,128]{2,1,0:T(8,128)S(1)}, f32[4,256,128]{2,1,0:T(8,128)S(1)}, u32[]{:S(2)}, u32[]{:S(2)}) %collective-permute-start.34) | collective-permute-done | bytes 524320 | tf_op jit(solution)/shard_map/ppermute | solution.py:18
  263.6 8.7 %collective-permute-done.36 = f32[4,256,128]{2,1,0:T(8,128)S(1)} collective-permute-done((f32[4,256,128]{2,1,0:T(8,128)S(1)}, f32[4,256,128]{2,1,0:T(8,128)S(1)}, u32[]{:S(2)}, u32[]{:S(2)}) %collective-permute-start.36) | collective-permute-done | bytes 524320 | tf_op jit(solution)/shard_map/ppermute | solution.py:18
  272.2 5.6 %collective-permute-done.37 = f32[4,256,128]{2,1,0:T(8,128)S(1)} collective-permute-done((f32[4,256,128]{2,1,0:T(8,128)S(1)}, f32[4,256,128]{2,1,0:T(8,128)S(1)}, u32[]{:S(2)}, u32[]{:S(2)}) %collective-permute-start.37) | collective-permute-done | bytes 524320 | tf_op jit(solution)/shard_map/ppermute | solution.py:18
  286.9 4.3 %fusion.23 = bf16[256,8,128]{2,0,1:T(8,128)(2,1)} fusion(f32[8,256,128]{2,1,0:T(8,128)} %fusion.119, f32[8,256,128]{2,1,0:T(8,128)} %fusion.118, f32[8,256,128]{2,1,0:T(8,128)} %fusion.117, f32[8,256,128]{2,1,0:T(8,128)} %fusion.116, f32[8,256,128]{2,1,0:T(8,128)} %fusion.115, f32[8,256,128]{2,1,0:T(8,128)} %fusion.114, f32[8,256,128]{2,1,0:T(8,128)S(1)} %copy-done.7, ...), kind=kOutput, calls=%fused_computation.57 | convolution fusion | flops 136577024 | bytes 9437184 | tf_op jit(solution)/shard_map/hqk,hqd->hkd/dot_general | solution.py:119
  294.5 5.6 %collective-permute-done.40 = f32[4,256,128]{2,1,0:T(8,128)} collective-permute-done((f32[4,256,128]{2,1,0:T(8,128)}, f32[4,256,128]{2,1,0:T(8,128)}, u32[]{:S(2)}, u32[]{:S(2)}) %collective-permute-start.40) | collective-permute-done | bytes 524320 | tf_op jit(solution)/shard_map/ppermute | solution.py:18
  (202 shorter events, 137.7 us)
Async XLA Ops:
  3.0 35.3 %collective-permute-start.14 = (bf16[8,256,128]{2,1,0:T(8,128)(2,1)}, bf16[8,256,128]{2,1,0:T(8,128)(2,1)}, u32[]{:S(2)}, u32[]{:S(2)}) collective-permute-start(bf16[8,256,128]{2,1,0:T(8,128)(2,1)} %bitcast.10), channel_id=1, source_target_pairs={{1,0},{2,1},{3,2},{4,3},{5,4},{6,5},{7,6},{8,7},{9,8},{10,9},{11,1... | collective-permute-start | bytes 1572872 | tf_op jit(solution)/shard_map/ppermute | solution.py:18
  55.3 14.7 %collective-permute-start.3 = (bf16[8,256,128]{2,1,0:T(8,128)(2,1)S(1)}, bf16[8,256,128]{2,1,0:T(8,128)(2,1)S(1)}, u32[]{:S(2)}, u32[]{:S(2)}) collective-permute-start(bf16[8,256,128]{2,1,0:T(8,128)(2,1)S(1)} %collective-permute-done.2), channel_id=1, source_target_pairs={{1,0},{2,1},{3,2},{4,3},{5,4},{6,5},{7,6},{8,7},{9,8},{10,9},{11,1... | collective-permute-start | bytes 1572872 | tf_op jit(solution)/shard_map/ppermute | solution.py:18
  66.2 14.7 %collective-permute-start.17 = (bf16[8,256,128]{2,1,0:T(8,128)(2,1)S(1)}, bf16[8,256,128]{2,1,0:T(8,128)(2,1)S(1)}, u32[]{:S(2)}, u32[]{:S(2)}) collective-permute-start(bf16[8,256,128]{2,1,0:T(8,128)(2,1)S(1)} %collective-permute-done.16), channel_id=1, source_target_pairs={{1,0},{2,1},{3,2},{4,3},{5,4},{6,5},{7,6},{8,7},{9,8},{10,9},{11,1... | collective-permute-start | bytes 1572872 | tf_op jit(solution)/shard_map/ppermute | solution.py:18
  70.0 14.7 %collective-permute-start.4 = (bf16[8,256,128]{2,1,0:T(8,128)(2,1)S(1)}, bf16[8,256,128]{2,1,0:T(8,128)(2,1)S(1)}, u32[]{:S(2)}, u32[]{:S(2)}) collective-permute-start(bf16[8,256,128]{2,1,0:T(8,128)(2,1)S(1)} %collective-permute-done.3), channel_id=1, source_target_pairs={{1,0},{2,1},{3,2},{4,3},{5,4},{6,5},{7,6},{8,7},{9,8},{10,9},{11,1... | collective-permute-start | bytes 1572872 | tf_op jit(solution)/shard_map/ppermute | solution.py:18
  80.9 14.7 %collective-permute-start.18 = (bf16[8,256,128]{2,1,0:T(8,128)(2,1)S(1)}, bf16[8,256,128]{2,1,0:T(8,128)(2,1)S(1)}, u32[]{:S(2)}, u32[]{:S(2)}) collective-permute-start(bf16[8,256,128]{2,1,0:T(8,128)(2,1)S(1)} %collective-permute-done.17), channel_id=1, source_target_pairs={{1,0},{2,1},{3,2},{4,3},{5,4},{6,5},{7,6},{8,7},{9,8},{10,9},{11,1... | collective-permute-start | bytes 1572872 | tf_op jit(solution)/shard_map/ppermute | solution.py:18
  84.7 14.7 %collective-permute-start.5 = (bf16[8,256,128]{2,1,0:T(8,128)(2,1)S(1)}, bf16[8,256,128]{2,1,0:T(8,128)(2,1)S(1)}, u32[]{:S(2)}, u32[]{:S(2)}) collective-permute-start(bf16[8,256,128]{2,1,0:T(8,128)(2,1)S(1)} %collective-permute-done.4), channel_id=1, source_target_pairs={{1,0},{2,1},{3,2},{4,3},{5,4},{6,5},{7,6},{8,7},{9,8},{10,9},{11,1... | collective-permute-start | bytes 1572872 | tf_op jit(solution)/shard_map/ppermute | solution.py:18
  99.4 14.7 %collective-permute-start.6 = (bf16[8,256,128]{2,1,0:T(8,128)(2,1)S(1)}, bf16[8,256,128]{2,1,0:T(8,128)(2,1)S(1)}, u32[]{:S(2)}, u32[]{:S(2)}) collective-permute-start(bf16[8,256,128]{2,1,0:T(8,128)(2,1)S(1)} %collective-permute-done.5), channel_id=1, source_target_pairs={{1,0},{2,1},{3,2},{4,3},{5,4},{6,5},{7,6},{8,7},{9,8},{10,9},{11,1... | collective-permute-start | bytes 1572872 | tf_op jit(solution)/shard_map/ppermute | solution.py:18
  122.4 50.8 %collective-permute-start.21 = (f32[4,256,128]{2,1,0:T(8,128)S(1)}, f32[4,256,128]{2,1,0:T(8,128)S(1)}, u32[]{:S(2)}, u32[]{:S(2)}) collective-permute-start(f32[4,256,128]{2,1,0:T(8,128)S(1)} %get-tuple-element.36), channel_id=1, source_target_pairs={{0,1},{1,2},{2,3},{3,4},{4,5},{5,6},{6,7},{7,8},{8,9},{9,10},{10,1... | collective-permute-start | bytes 1572872 | tf_op jit(solution)/shard_map/ppermute | solution.py:18
  125.0 48.3 %collective-permute-start.22 = (f32[4,256,128]{2,1,0:T(8,128)S(1)}, f32[4,256,128]{2,1,0:T(8,128)S(1)}, u32[]{:S(2)}, u32[]{:S(2)}) collective-permute-start(f32[4,256,128]{2,1,0:T(8,128)S(1)} %get-tuple-element.37), channel_id=1, source_target_pairs={{0,1},{1,2},{2,3},{3,4},{4,5},{5,6},{6,7},{7,8},{8,9},{9,10},{10,1... | collective-permute-start | bytes 1572872 | tf_op jit(solution)/shard_map/ppermute | solution.py:18
  126.9 16.1 %collective-permute-start.26 = (f32[8,256]{1,0:T(8,128)S(1)}, f32[8,256]{1,0:T(8,128)S(1)}, u32[]{:S(2)}, u32[]{:S(2)}) collective-permute-start(f32[8,256]{1,0:T(8,128)S(1)} %add_select_fusion.6), channel_id=1, source_target_pairs={{0,1},{1,2},{2,3},{3,4},{4,5},{5,6},{6,7},{7,8},{8,9},{9,10},{10,1... | collective-permute-start | bytes 24584 | tf_op jit(solution)/shard_map/ppermute | solution.py:18
  170.6 28.0 %collective-permute-start.38 = (f32[8,256]{1,0:T(8,128)S(1)}, f32[8,256]{1,0:T(8,128)S(1)}, u32[]{:S(2)}, u32[]{:S(2)}) collective-permute-start(f32[8,256]{1,0:T(8,128)S(1)} %add_select_fusion.2), channel_id=1, source_target_pairs={{0,1},{1,2},{2,3},{3,4},{4,5},{5,6},{6,7},{7,8},{8,9},{9,10},{10,1... | collective-permute-start | bytes 24584 | tf_op jit(solution)/shard_map/ppermute | solution.py:18
  173.8 14.7 %collective-permute-start.24 = (f32[4,256,128]{2,1,0:T(8,128)S(1)}, f32[4,256,128]{2,1,0:T(8,128)S(1)}, u32[]{:S(2)}, u32[]{:S(2)}) collective-permute-start(f32[4,256,128]{2,1,0:T(8,128)S(1)} %get-tuple-element.34), channel_id=1, source_target_pairs={{0,1},{1,2},{2,3},{3,4},{4,5},{5,6},{6,7},{7,8},{8,9},{9,10},{10,1... | collective-permute-start | bytes 1572872 | tf_op jit(solution)/shard_map/ppermute | solution.py:18
  175.8 18.4 %collective-permute-start.25 = (f32[4,256,128]{2,1,0:T(8,128)S(1)}, f32[4,256,128]{2,1,0:T(8,128)S(1)}, u32[]{:S(2)}, u32[]{:S(2)}) collective-permute-start(f32[4,256,128]{2,1,0:T(8,128)S(1)} %get-tuple-element.35), channel_id=1, source_target_pairs={{0,1},{1,2},{2,3},{3,4},{4,5},{5,6},{6,7},{7,8},{8,9},{9,10},{10,1... | collective-permute-start | bytes 1572872 | tf_op jit(solution)/shard_map/ppermute | solution.py:18
  194.7 14.7 %collective-permute-start.27 = (f32[4,256,128]{2,1,0:T(8,128)S(1)}, f32[4,256,128]{2,1,0:T(8,128)S(1)}, u32[]{:S(2)}, u32[]{:S(2)}) collective-permute-start(f32[4,256,128]{2,1,0:T(8,128)S(1)} %get-tuple-element.32), channel_id=1, source_target_pairs={{0,1},{1,2},{2,3},{3,4},{4,5},{5,6},{6,7},{7,8},{8,9},{9,10},{10,1... | collective-permute-start | bytes 1572872 | tf_op jit(solution)/shard_map/ppermute | solution.py:18
  196.7 18.4 %collective-permute-start.28 = (f32[4,256,128]{2,1,0:T(8,128)S(1)}, f32[4,256,128]{2,1,0:T(8,128)S(1)}, u32[]{:S(2)}, u32[]{:S(2)}) collective-permute-start(f32[4,256,128]{2,1,0:T(8,128)S(1)} %get-tuple-element.33), channel_id=1, source_target_pairs={{0,1},{1,2},{2,3},{3,4},{4,5},{5,6},{6,7},{7,8},{8,9},{9,10},{10,1... | collective-permute-start | bytes 1572872 | tf_op jit(solution)/shard_map/ppermute | solution.py:18
  198.6 41.8 %collective-permute-start.41 = (f32[8,256]{1,0:T(8,128)S(1)}, f32[8,256]{1,0:T(8,128)S(1)}, u32[]{:S(2)}, u32[]{:S(2)}) collective-permute-start(f32[8,256]{1,0:T(8,128)S(1)} %add_select_fusion.1), channel_id=1, source_target_pairs={{0,1},{1,2},{2,3},{3,4},{4,5},{5,6},{6,7},{7,8},{8,9},{9,10},{10,1... | collective-permute-start | bytes 24584 | tf_op jit(solution)/shard_map/ppermute | solution.py:18
  215.7 14.7 %collective-permute-start.30 = (f32[4,256,128]{2,1,0:T(8,128)S(1)}, f32[4,256,128]{2,1,0:T(8,128)S(1)}, u32[]{:S(2)}, u32[]{:S(2)}) collective-permute-start(f32[4,256,128]{2,1,0:T(8,128)S(1)} %get-tuple-element.30), channel_id=1, source_target_pairs={{0,1},{1,2},{2,3},{3,4},{4,5},{5,6},{6,7},{7,8},{8,9},{9,10},{10,1... | collective-permute-start | bytes 1572872 | tf_op jit(solution)/shard_map/ppermute | solution.py:18
  217.6 18.4 %collective-permute-start.31 = (f32[4,256,128]{2,1,0:T(8,128)S(1)}, f32[4,256,128]{2,1,0:T(8,128)S(1)}, u32[]{:S(2)}, u32[]{:S(2)}) collective-permute-start(f32[4,256,128]{2,1,0:T(8,128)S(1)} %get-tuple-element.31), channel_id=1, source_target_pairs={{0,1},{1,2},{2,3},{3,4},{4,5},{5,6},{6,7},{7,8},{8,9},{9,10},{10,1... | collective-permute-start | bytes 1572872 | tf_op jit(solution)/shard_map/ppermute | solution.py:18
  236.6 14.7 %collective-permute-start.33 = (f32[4,256,128]{2,1,0:T(8,128)S(1)}, f32[4,256,128]{2,1,0:T(8,128)S(1)}, u32[]{:S(2)}, u32[]{:S(2)}) collective-permute-start(f32[4,256,128]{2,1,0:T(8,128)S(1)} %get-tuple-element.28), channel_id=1, source_target_pairs={{0,1},{1,2},{2,3},{3,4},{4,5},{5,6},{6,7},{7,8},{8,9},{9,10},{10,1... | collective-permute-start | bytes 1572872 | tf_op jit(solution)/shard_map/ppermute | solution.py:18
  238.5 18.4 %collective-permute-start.34 = (f32[4,256,128]{2,1,0:T(8,128)S(1)}, f32[4,256,128]{2,1,0:T(8,128)S(1)}, u32[]{:S(2)}, u32[]{:S(2)}) collective-permute-start(f32[4,256,128]{2,1,0:T(8,128)S(1)} %get-tuple-element.29), channel_id=1, source_target_pairs={{0,1},{1,2},{2,3},{3,4},{4,5},{5,6},{6,7},{7,8},{8,9},{9,10},{10,1... | collective-permute-start | bytes 1572872 | tf_op jit(solution)/shard_map/ppermute | solution.py:18
  257.5 14.7 %collective-permute-start.36 = (f32[4,256,128]{2,1,0:T(8,128)S(1)}, f32[4,256,128]{2,1,0:T(8,128)S(1)}, u32[]{:S(2)}, u32[]{:S(2)}) collective-permute-start(f32[4,256,128]{2,1,0:T(8,128)S(1)} %get-tuple-element.26), channel_id=1, source_target_pairs={{0,1},{1,2},{2,3},{3,4},{4,5},{5,6},{6,7},{7,8},{8,9},{9,10},{10,1... | collective-permute-start | bytes 1572872 | tf_op jit(solution)/shard_map/ppermute | solution.py:18
  259.4 18.4 %collective-permute-start.37 = (f32[4,256,128]{2,1,0:T(8,128)S(1)}, f32[4,256,128]{2,1,0:T(8,128)S(1)}, u32[]{:S(2)}, u32[]{:S(2)}) collective-permute-start(f32[4,256,128]{2,1,0:T(8,128)S(1)} %get-tuple-element.27), channel_id=1, source_target_pairs={{0,1},{1,2},{2,3},{3,4},{4,5},{5,6},{6,7},{7,8},{8,9},{9,10},{10,1... | collective-permute-start | bytes 1572872 | tf_op jit(solution)/shard_map/ppermute | solution.py:18
  279.4 15.2 %collective-permute-start.39 = (f32[4,256,128]{2,1,0:T(8,128)}, f32[4,256,128]{2,1,0:T(8,128)}, u32[]{:S(2)}, u32[]{:S(2)}) collective-permute-start(f32[4,256,128]{2,1,0:T(8,128)} %get-tuple-element.24), channel_id=1, source_target_pairs={{0,1},{1,2},{2,3},{3,4},{4,5},{5,6},{6,7},{7,8},{8,9},{9,10},{10,1... | collective-permute-start | bytes 1572872 | tf_op jit(solution)/shard_map/ppermute | solution.py:18
  281.4 18.7 %collective-permute-start.40 = (f32[4,256,128]{2,1,0:T(8,128)}, f32[4,256,128]{2,1,0:T(8,128)}, u32[]{:S(2)}, u32[]{:S(2)}) collective-permute-start(f32[4,256,128]{2,1,0:T(8,128)} %get-tuple-element.25), channel_id=1, source_target_pairs={{0,1},{1,2},{2,3},{3,4},{4,5},{5,6},{6,7},{7,8},{8,9},{9,10},{10,1... | collective-permute-start | bytes 1572872 | tf_op jit(solution)/shard_map/ppermute | solution.py:18
  (37 other events, 556.1 us)

commit v2 on v0

v2 whole, which is shorter than its diff:
```python
import math

import jax
import jax.numpy as jnp
from jax import lax
from jax.sharding import PartitionSpec as P

HEADS = 8
DH = 128
BLOCK = 128
REACH = 7


def from_behind(value, axis, steps):
    count = lax.axis_size(axis)
    first, last = (max(0, -steps), min(count, count - steps))
    return lax.ppermute(value, axis, [(source, source + steps) for source in range(first, last)])


def doc_window(doc_blocks, first_block, count):
    ends = jnp.cumsum(doc_blocks)
    starts = ends - doc_blocks
    block_ids = first_block + jnp.arange(count, dtype=jnp.int32)
    found = jnp.sum((starts[None, :] <= block_ids[:, None]).astype(jnp.int32), axis=1) - 1
    return jnp.where(block_ids >= ends[-1], -2, found)


def per_device(query_rows, key_rows, value_rows, forward_out, out_grad, doc_blocks):
    rows, features = query_rows.shape
    scale = 1.0 / math.sqrt(DH)
    axes = ("cx", "cy")
    shard = lax.axis_index(axes)
    per_shard = rows // BLOCK
    window = REACH + 1
    block_docs = doc_window(doc_blocks, (shard - REACH) * per_shard, (2 * REACH + 1) * per_shard)
    token_docs = jnp.repeat(block_docs, BLOCK)

    def docs_at(step):
        return token_docs[(REACH + step) * rows : (REACH + step + 1) * rows]

    local_docs = docs_at(0)
    offsets = jnp.arange(rows, dtype=jnp.int32)
    causal = offsets[None, :] <= offsets[:, None]
    query_masks = [local_docs[:, None] == docs_at(-step)[None, :] for step in range(window)]
    query_masks[0] = query_masks[0] & causal
    key_masks = [docs_at(step)[:, None] == local_docs[None, :] for step in range(window)]

    def to_heads(x):
        return x.reshape(rows, HEADS, DH).transpose(1, 0, 2)

    def from_heads(x):
        return x.transpose(1, 0, 2).reshape(rows, features)

    query_h = to_heads(query_rows)
    grad_h = to_heads(out_grad)
    key_h = to_heads(key_rows)
    value_h = to_heads(value_rows)
    delta = jnp.einsum(
        "hqd,hqd->hq", grad_h, to_heads(forward_out), preferred_element_type=jnp.float32
    )

    key_values = [(key_h, value_h)]
    query_grads = [(query_h, grad_h)]
    moving_kv = (key_h, value_h)
    moving_qg = (query_h, grad_h)
    for step in range(1, window):
        moving_kv = from_behind(moving_kv, axes, 1)
        moving_qg = from_behind(moving_qg, axes, -1)
        key_values.append(moving_kv)
        query_grads.append(moving_qg)

    def scores_of(q, k, mask):
        s = jnp.einsum("hqd,hkd->hqk", q, k, preferred_element_type=jnp.float32) * scale
        return jnp.where(mask[None], s, -1e30)

    def tile_stats(q, k, mask):
        s = scores_of(q, k, mask)
        top = jnp.max(s, axis=2)
        return (top, jnp.sum(jnp.exp(s - top[..., None]), axis=2))

    stats = tile_stats(query_h, key_h, query_masks[0])
    for step in range(1, window):
        part = tile_stats(query_h, key_values[step][0], query_masks[step])
        top = jnp.maximum(stats[0], part[0])
        total = stats[1] * jnp.exp(stats[0] - top) + part[1] * jnp.exp(part[0] - top)
        stats = (top, total)
    logsum = stats[0] + jnp.log(stats[1])

    row_stats = jnp.concatenate([logsum, delta], axis=1)
    later_stats = [row_stats] + [from_behind(row_stats, axes, -step) for step in range(1, window)]

    def tile_grads(q, g, k, v, lse, dlt, mask):
        s = scores_of(q, k, mask)
        prob = jnp.where(mask[None], jnp.exp(s - lse[..., None]), 0.0)
        dprob = jnp.einsum("hqd,hkd->hqk", g, v, preferred_element_type=jnp.float32)
        dscore = (prob * (dprob - dlt[..., None])).astype(jnp.bfloat16)
        return prob.astype(jnp.bfloat16), dscore

    prob_b, dscore = tile_grads(query_h, grad_h, key_h, value_h, logsum, delta, query_masks[0])
    query_acc = jnp.einsum("hqk,hkd->hqd", dscore, key_h, preferred_element_type=jnp.float32)
    key_acc = jnp.einsum("hqk,hqd->hkd", dscore, query_h, preferred_element_type=jnp.float32)
    value_acc = jnp.einsum("hqk,hqd->hkd", prob_b, grad_h, preferred_element_type=jnp.float32)
    for step in range(1, window):
        k_in, v_in = key_values[step]
        _, dscore = tile_grads(query_h, grad_h, k_in, v_in, logsum, delta, query_masks[step])
        query_acc = query_acc + jnp.einsum(
            "hqk,hkd->hqd", dscore, k_in, preferred_element_type=jnp.float32
        )
        q_in, g_in = query_grads[step]
        lse_in = later_stats[step][:, :rows]
        delta_in = later_stats[step][:, rows:]
        prob_b, dscore = tile_grads(q_in, g_in, key_h, value_h, lse_in, delta_in, key_masks[step])
        key_acc = key_acc + jnp.einsum(
            "hqk,hqd->hkd", dscore, q_in, preferred_element_type=jnp.float32
        )
        value_acc = value_acc + jnp.einsum(
            "hqk,hqd->hkd", prob_b, g_in, preferred_element_type=jnp.float32
        )
    query_grad = from_heads(query_acc * scale).astype(jnp.bfloat16)
    key_grad = from_heads(key_acc * scale).astype(jnp.bfloat16)
    value_grad = from_heads(value_acc).astype(jnp.bfloat16)
    return (query_grad, key_grad, value_grad)


def solution(mesh):
    in_specs = (
        P(("cx", "cy"), None),
        P(("cx", "cy"), None),
        P(("cx", "cy"), None),
        P(("cx", "cy"), None),
        P(("cx", "cy"), None),
        P(),
    )
    out_specs = (P(("cx", "cy"), None), P(("cx", "cy"), None), P(("cx", "cy"), None))
    return jax.shard_map(
        per_device, mesh=mesh, in_specs=in_specs, out_specs=out_specs, check_vma=False
    )
```

time: 326 us -> 256 us (0.79)
  the two profiles are of different devices: /device:TPU:6 before, /device:TPU:14 now
where the time goes in v2:
time: 256 us; the launch traced here: 254 us
  starting transfers between devices  123 us (48%)
  matrix products  94.9 us (37%)
  local copies, waits for them, and re-layouts  19 us (7%)
  waiting for transfers between devices  7.35 us (3%)
  other arithmetic  6.97 us (3%)
    ppermute x35, starting transfers between devices, from_behind(): lax.ppermute(value, axis, [(source, source + steps) for source in range(f...  123 us
    dot_general x7, matrix products, per_device(): jnp.einsum('hqk,hqd->hkd', dscore, q_in, preferred_element_type=jnp.float32)  27.8 us
    dot_general x7, matrix products, per_device(): jnp.einsum('hqk,hkd->hqd', dscore, k_in, preferred_element_type=jnp.float32)  26.8 us
    dot_general x15, matrix products, scores_of(): jnp.einsum('hqd,hkd->hqk', q, k, preferred_element_type=jnp.float32) * scale  25.2 us
    unnamed x140, local copies, waits for them, and re-layouts  13.5 us
    dot_general x7, matrix products, per_device(): jnp.einsum('hqk,hqd->hkd', prob_b, g_in, preferred_element_type=jnp.float32)  9.08 us
    ppermute x35, waiting for transfers between devices, from_behind(): lax.ppermute(value, axis, [(source, source + steps) for source in range(f...  7.35 us
  transfers between devices with their start and end apart: 35, of which 4 were waited for; matrix products, arithmetic and copies ran while one was open for 38% of the time, Pallas kernels for 0%

profile of v2, /device:TPU:14, one launch (start us, length us, event | category | flops | bytes accessed | tf_op | source)
XLA Modules:
  0.0 253.6 jit_solution(16809204490256066564)
XLA Ops:
  5.6 4.0 %collective-permute-start.7 = (bf16[8,256,128]{2,1,0:T(8,128)(2,1)}, bf16[8,256,128]{2,1,0:T(8,128)(2,1)}, u32[]{:S(2)}, u32[]{:S(2)}) collective-permute-start(bf16[8,256,128]{2,1,0:T(8,128)(2,1)} %bitcast.17), channel_id=1, source_target_pairs={{0,1},{1,2},{2,3},{3,4},{4,5},{5,6},{6,7},{7,8},{8,9},{9,10},{10,1... | collective-permute-start | bytes 1572872 | tf_op jit(solution)/shard_map/ppermute | solution.py:17
  10.1 5.1 %collective-permute-start.14 = (bf16[8,256,128]{2,1,0:T(8,128)(2,1)S(1)}, bf16[8,256,128]{2,1,0:T(8,128)(2,1)}, u32[]{:S(2)}, u32[]{:S(2)}) collective-permute-start(bf16[8,256,128]{2,1,0:T(8,128)(2,1)S(1)} %bitcast.210), channel_id=1, source_target_pairs={{1,0},{2,1},{3,2},{4,3},{5,4},{6,5},{7,6},{8,7},{9,8},{10,9},{11,1... | collective-permute-start | bytes 1572872 | tf_op jit(solution)/shard_map/ppermute | solution.py:17
  27.7 5.8 %collective-permute-start.17 = (bf16[8,256,128]{2,1,0:T(8,128)(2,1)}, bf16[8,256,128]{2,1,0:T(8,128)(2,1)}, u32[]{:S(2)}, u32[]{:S(2)}) collective-permute-start(bf16[8,256,128]{2,1,0:T(8,128)(2,1)} %collective-permute-done.14), channel_id=1, source_target_pairs={{1,0},{2,1},{3,2},{4,3},{5,4},{6,5},{7,6},{8,7},{9,8},{10,9},{11,1... | collective-permute-start | bytes 1572872 | tf_op jit(solution)/shard_map/ppermute | solution.py:17
  43.8 5.8 %collective-permute-start.20 = (bf16[8,256,128]{2,1,0:T(8,128)(2,1)}, bf16[8,256,128]{2,1,0:T(8,128)(2,1)S(1)}, u32[]{:S(2)}, u32[]{:S(2)}) collective-permute-start(bf16[8,256,128]{2,1,0:T(8,128)(2,1)} %collective-permute-done.17), channel_id=1, source_target_pairs={{1,0},{2,1},{3,2},{4,3},{5,4},{6,5},{7,6},{8,7},{9,8},{10,9},{11,1... | collective-permute-start | bytes 1572872 | tf_op jit(solution)/shard_map/ppermute | solution.py:17
  60.2 5.8 %collective-permute-start.23 = (bf16[8,256,128]{2,1,0:T(8,128)(2,1)S(1)}, bf16[8,256,128]{2,1,0:T(8,128)(2,1)S(1)}, u32[]{:S(2)}, u32[]{:S(2)}) collective-permute-start(bf16[8,256,128]{2,1,0:T(8,128)(2,1)S(1)} %collective-permute-done.20), channel_id=1, source_target_pairs={{1,0},{2,1},{3,2},{4,3},{5,4},{6,5},{7,6},{8,7},{9,8},{10,9},{11,1... | collective-permute-start | bytes 1572872 | tf_op jit(solution)/shard_map/ppermute | solution.py:17
  74.5 5.8 %collective-permute-start.26 = (bf16[8,256,128]{2,1,0:T(8,128)(2,1)S(1)}, bf16[8,256,128]{2,1,0:T(8,128)(2,1)S(1)}, u32[]{:S(2)}, u32[]{:S(2)}) collective-permute-start(bf16[8,256,128]{2,1,0:T(8,128)(2,1)S(1)} %collective-permute-done.23), channel_id=1, source_target_pairs={{1,0},{2,1},{3,2},{4,3},{5,4},{6,5},{7,6},{8,7},{9,8},{10,9},{11,1... | collective-permute-start | bytes 1572872 | tf_op jit(solution)/shard_map/ppermute | solution.py:17
  80.3 3.9 %collective-permute-start.28 = (bf16[8,256,128]{2,1,0:T(8,128)(2,1)S(1)}, bf16[8,256,128]{2,1,0:T(8,128)(2,1)S(1)}, u32[]{:S(2)}, u32[]{:S(2)}) collective-permute-start(bf16[8,256,128]{2,1,0:T(8,128)(2,1)S(1)} %collective-permute-done.25), channel_id=1, source_target_pairs={{1,0},{2,1},{3,2},{4,3},{5,4},{6,5},{7,6},{8,7},{9,8},{10,9},{11,1... | collective-permute-start | bytes 1572872 | tf_op jit(solution)/shard_map/ppermute | solution.py:17
  90.5 5.8 %collective-permute-start.29 = (bf16[8,256,128]{2,1,0:T(8,128)(2,1)S(1)}, bf16[8,256,128]{2,1,0:T(8,128)(2,1)}, u32[]{:S(2)}, u32[]{:S(2)}) collective-permute-start(bf16[8,256,128]{2,1,0:T(8,128)(2,1)S(1)} %collective-permute-done.26), channel_id=1, source_target_pairs={{1,0},{2,1},{3,2},{4,3},{5,4},{6,5},{7,6},{8,7},{9,8},{10,9},{11,1... | collective-permute-start | bytes 1572872 | tf_op jit(solution)/shard_map/ppermute | solution.py:17
  106.3 5.8 %collective-permute-start.32 = (bf16[8,256,128]{2,1,0:T(8,128)(2,1)}, bf16[8,256,128]{2,1,0:T(8,128)(2,1)}, u32[]{:S(2)}, u32[]{:S(2)}) collective-permute-start(bf16[8,256,128]{2,1,0:T(8,128)(2,1)} %collective-permute-done.29), channel_id=1, source_target_pairs={{1,0},{2,1},{3,2},{4,3},{5,4},{6,5},{7,6},{8,7},{9,8},{10,9},{11,1... | collective-permute-start | bytes 1572872 | tf_op jit(solution)/shard_map/ppermute | solution.py:17
  125.5 4.1 %fusion.3 = f32[8,256,128]{1,2,0:T(8,128)} fusion(f32[8,256,128]{1,2,0:T(8,128)} %fusion.173, bf16[8,256,128]{2,1,0:T(8,128)(2,1)} %collective-permute-done, f32[8,256,256]{1,2,0:T(8,128)} %copy-done, bf16[8,256,128]{2,1,0:T(8,128)(2,1)} %collective-permute-done.7, f32[8,256]{1,0:T(8,128)S(1)} %copy.288, f32[8,256]{1,0:T(8,128)S(1)} %log_add_fusion, ...), kind=kOutput, calls=%fused_computation.42 | convolution fusion | flops 271319040 | bytes 5849088 | tf_op jit(solution)/shard_map/hqk,hkd->hqd/dot_general | solution.py:106
  129.6 4.0 %fusion.5 = f32[8,256,128]{1,2,0:T(8,128)} fusion(f32[8,256,128]{1,2,0:T(8,128)} %fusion.3, bf16[8,256,128]{2,1,0:T(8,128)(2,1)} %collective-permute-done.1, f32[8,256,256]{1,2,0:T(8,128)} %copy-done.1, bf16[8,256,128]{2,1,0:T(8,128)(2,1)} %collective-permute-done.8, f32[8,256]{1,0:T(8,128)S(1)} %copy.288, f32[8,256]{1,0:T(8,128)S(1)} %log_add_fusion, ...), kind=kOutput, calls=%fused_computation.44 | convolution fusion | flops 271319040 | bytes 5849088 | tf_op jit(solution)/shard_map/hqk,hkd->hqd/dot_general | solution.py:106
  133.7 4.1 %fusion.7 = f32[8,256,128]{1,2,0:T(8,128)} fusion(f32[8,256,128]{1,2,0:T(8,128)} %fusion.5, bf16[8,256,128]{2,1,0:T(8,128)(2,1)} %collective-permute-done.2, f32[8,256,256]{1,2,0:T(8,128)} %copy-done.2, bf16[8,256,128]{2,1,0:T(8,128)(2,1)} %copy-done.40, f32[8,256]{1,0:T(8,128)S(1)} %copy.288, f32[8,256]{1,0:T(8,128)S(1)} %log_add_fusion, ...), kind=kOutput, calls=%fused_computation.46 | convolution fusion | flops 271319040 | bytes 5849088 | tf_op jit(solution)/shard_map/hqk,hkd->hqd/dot_general | solution.py:106
  137.8 3.9 %fusion.9 = f32[8,256,128]{1,2,0:T(8,128)} fusion(f32[8,256,128]{1,2,0:T(8,128)} %fusion.7, bf16[8,256,128]{2,1,0:T(8,128)(2,1)S(1)} %copy-done.28, f32[8,256,256]{1,2,0:T(8,128)} %copy-done.3, bf16[8,256,128]{2,1,0:T(8,128)(2,1)} %copy-done.41, f32[8,256]{1,0:T(8,128)S(1)} %copy.288, f32[8,256]{1,0:T(8,128)S(1)} %log_add_fusion, ...), kind=kOutput, calls=%fused_computation.48 | convolution fusion | flops 271319040 | bytes 5849088 | tf_op jit(solution)/shard_map/hqk,hkd->hqd/dot_general | solution.py:106
  141.7 4.1 %fusion.11 = f32[8,256,128]{1,2,0:T(8,128)} fusion(f32[8,256,128]{1,2,0:T(8,128)} %fusion.9, bf16[8,256,128]{2,1,0:T(8,128)(2,1)} %copy-done.29, f32[8,256,256]{1,2,0:T(8,128)} %copy-done.4, bf16[8,256,128]{2,1,0:T(8,128)(2,1)} %copy-done.42, f32[8,256]{1,0:T(8,128)S(1)} %copy.288, f32[8,256]{1,0:T(8,128)S(1)} %log_add_fusion, ...), kind=kOutput, calls=%fused_computation.50 | convolution fusion | flops 271319040 | bytes 5849088 | tf_op jit(solution)/shard_map/hqk,hkd->hqd/dot_general | solution.py:106
  152.4 3.5 %fusion.20 = bf16[8,256,128]{1,2,0:T(8,128)(2,1)} fusion(f32[8,256,128]{1,2,0:T(8,128)S(1)} %fusion.13, bf16[8,256,128]{2,1,0:T(8,128)(2,1)} %copy-done.43, f32[8,256,256]{1,2,0:T(8,128)} %copy-done.10, bf16[8,256,128]{2,1,0:T(8,128)(2,1)} %collective-permute-done.13, f32[8,256]{1,0:T(8,128)S(1)} %copy.288, f32[8,256]{1,0:T(8,128)S(1)} %log_add_fusion, ...), kind=kOutput, calls=%fused_computation.72 | convolution fusion | flops 271843328 | bytes 5324800 | tf_op jit(solution)/shard_map/hqk,hkd->hqd/dot_general | solution.py:106
  158.4 4.7 %collective-permute-start.24 = (f32[8,512]{1,0:T(8,128)}, f32[8,512]{1,0:T(8,128)S(1)}, u32[]{:S(2)}, u32[]{:S(2)}) collective-permute-start(f32[8,512]{1,0:T(8,128)} %pad_maximum_fusion), channel_id=1, source_target_pairs={{4,0},{5,1},{6,2},{7,3},{8,4},{9,5},{10,6},{11,7},{12,8},{13,9},{1... | collective-permute-start | bytes 49160 | tf_op jit(solution)/shard_map/ppermute | solution.py:17
  163.9 21.1 %collective-permute-start.27 = (f32[8,512]{1,0:T(8,128)}, f32[8,512]{1,0:T(8,128)S(1)}, u32[]{:S(2)}, u32[]{:S(2)}) collective-permute-start(f32[8,512]{1,0:T(8,128)} %pad_maximum_fusion), channel_id=1, source_target_pairs={{5,0},{6,1},{7,2},{8,3},{9,4},{10,5},{11,6},{12,7},{13,8},{14,9},{... | collective-permute-start | bytes 49160 | tf_op jit(solution)/shard_map/ppermute | solution.py:17
  202.7 3.8 %fusion.19 = f32[8,256,128]{1,2,0:T(8,128)} fusion(f32[8,256,128]{1,2,0:T(8,128)} %fusion.172, bf16[8,256,128]{2,1,0:T(8,128)(2,1)} %collective-permute-done.14, bf16[8,256,128]{2,1,0:T(8,128)(2,1)} %collective-permute-done.16, f32[8,256,256]{1,2,0:T(8,128)S(1)} %copy-done.8, f32[8,256]{1,0:T(8,128)S(1)} %get-tuple-element.28, ...), kind=kOutput, calls=%fused_computation.71 | convolution fusion | flops 272367616 | bytes 5849088 | tf_op jit(solution)/shard_map/hqk,hqd->hkd/dot_general | solution.py:113
  206.4 4.1 %convolution_add_fusion.12 = f32[8,256,128]{1,2,0:T(8,128)} fusion(f32[8,256,128]{1,2,0:T(8,128)} %fusion.19, bf16[8,256,128]{2,1,0:T(8,128)(2,1)} %collective-permute-done.17, f32[8,256,256]{1,2,0:T(8,128)} %exponential_select_fusion.5, bf16[8,256,128]{2,1,0:T(8,128)(2,1)} %collective-permute-done.19, f32[8,256]{1,0:T(8,128)S(1)} %get-tuple-element.25, ...), kind=kOutput, calls=%fused_computation.69 | convolution fusion | flops 270270464 | bytes 5775360 | tf_op jit(solution)/shard_map/hqk,hqd->hkd/dot_general | solution.py:113
  210.5 3.9 %convolution_add_fusion.11 = f32[8,256,128]{1,2,0:T(8,128)} fusion(f32[8,256,128]{1,2,0:T(8,128)} %convolution_add_fusion.12, bf16[8,256,128]{2,1,0:T(8,128)(2,1)} %copy-done.48, f32[8,256,256]{1,2,0:T(8,128)} %exponential_select_fusion.4, bf16[8,256,128]{2,1,0:T(8,128)(2,1)S(1)} %copy-done.32, f32[8,256]{1,0:T(8,128)S(1)} %get-tuple-element.23, ...), kind=kOutput, calls=%fused_computation.68 | convolution fusion | flops 270270464 | bytes 5775360 | tf_op jit(solution)/shard_map/hqk,hqd->hkd/dot_general | solution.py:113
  214.4 4.1 %convolution_add_fusion.10 = f32[8,256,128]{1,2,0:T(8,128)} fusion(f32[8,256,128]{1,2,0:T(8,128)} %convolution_add_fusion.11, bf16[8,256,128]{2,1,0:T(8,128)(2,1)} %copy-done.50, f32[8,256,256]{1,2,0:T(8,128)} %exponential_select_fusion.3, bf16[8,256,128]{2,1,0:T(8,128)(2,1)} %copy-done.34, f32[8,256]{1,0:T(8,128)S(1)} %get-tuple-element.21, ...), kind=kOutput, calls=%fused_computation.67 | convolution fusion | flops 270270464 | bytes 5775360 | tf_op jit(solution)/shard_map/hqk,hqd->hkd/dot_general | solution.py:113
  221.7 3.9 %convolution_add_fusion.9 = f32[8,256,128]{1,2,0:T(8,128)} fusion(f32[8,256,128]{1,2,0:T(8,128)} %convolution_add_fusion.10, bf16[8,256,128]{2,1,0:T(8,128)(2,1)} %copy-done.52, f32[8,256,256]{1,2,0:T(8,128)} %exponential_select_fusion.2, bf16[8,256,128]{2,1,0:T(8,128)(2,1)S(1)} %copy-done.37, f32[8,256]{1,0:T(8,128)S(1)} %get-tuple-element.19, ...), kind=kOutput, calls=%fused_computation.66 | convolution fusion | flops 270270464 | bytes 5775360 | tf_op jit(solution)/shard_map/hqk,hqd->hkd/dot_general | solution.py:113
  228.7 4.1 %convolution_add_fusion.8 = f32[8,256,128]{1,2,0:T(8,128)} fusion(f32[8,256,128]{1,2,0:T(8,128)} %convolution_add_fusion.9, bf16[8,256,128]{2,1,0:T(8,128)(2,1)} %collective-permute-done.29, f32[8,256,256]{1,2,0:T(8,128)} %exponential_select_fusion.1, bf16[8,256,128]{2,1,0:T(8,128)(2,1)} %collective-permute-done.31, f32[8,256]{1,0:T(8,128)S(1)} %get-tuple-element.17, ...), kind=kOutput, calls=%fused_computation.65 | convolution fusion | flops 270270464 | bytes 5775360 | tf_op jit(solution)/shard_map/hqk,hqd->hkd/dot_general | solution.py:113
  232.8 4.0 %fusion.22 = bf16[8,256,128]{1,2,0:T(8,128)(2,1)} fusion(f32[8,256,128]{1,2,0:T(8,128)} %convolution_add_fusion.8, bf16[8,256,128]{2,1,0:T(8,128)(2,1)} %collective-permute-done.32, f32[8,256,256]{1,2,0:T(8,128)} %exponential_select_fusion, bf16[8,256,128]{2,1,0:T(8,128)(2,1)} %collective-permute-done.34, f32[8,256]{1,0:T(8,128)S(1)} %get-tuple-element.15, ...), kind=kOutput, calls=%fused_computation.74 | convolution fusion | flops 270794752 | bytes 5251072 | tf_op jit(solution)/shard_map/hqk,hqd->hkd/dot_general | solution.py:113
  (268 shorter events, 126.8 us)
Async XLA Ops:
  2.3 21.0 %collective-permute-start = (bf16[8,256,128]{2,1,0:T(8,128)(2,1)S(1)}, bf16[8,256,128]{2,1,0:T(8,128)(2,1)}, u32[]{:S(2)}, u32[]{:S(2)}) collective-permute-start(bf16[8,256,128]{2,1,0:T(8,128)(2,1)S(1)} %bitcast.218), channel_id=1, source_target_pairs={{0,1},{1,2},{2,3},{3,4},{4,5},{5,6},{6,7},{7,8},{8,9},{9,10},{10,1... | collective-permute-start | bytes 1572872 | tf_op jit(solution)/shard_map/ppermute | solution.py:17
  5.6 20.2 %collective-permute-start.7 = (bf16[8,256,128]{2,1,0:T(8,128)(2,1)}, bf16[8,256,128]{2,1,0:T(8,128)(2,1)}, u32[]{:S(2)}, u32[]{:S(2)}) collective-permute-start(bf16[8,256,128]{2,1,0:T(8,128)(2,1)} %bitcast.17), channel_id=1, source_target_pairs={{0,1},{1,2},{2,3},{3,4},{4,5},{5,6},{6,7},{7,8},{8,9},{9,10},{10,1... | collective-permute-start | bytes 1572872 | tf_op jit(solution)/shard_map/ppermute | solution.py:17
  10.1 17.5 %collective-permute-start.14 = (bf16[8,256,128]{2,1,0:T(8,128)(2,1)S(1)}, bf16[8,256,128]{2,1,0:T(8,128)(2,1)}, u32[]{:S(2)}, u32[]{:S(2)}) collective-permute-start(bf16[8,256,128]{2,1,0:T(8,128)(2,1)S(1)} %bitcast.210), channel_id=1, source_target_pairs={{1,0},{2,1},{3,2},{4,3},{5,4},{6,5},{7,6},{8,7},{9,8},{10,9},{11,1... | collective-permute-start | bytes 1572872 | tf_op jit(solution)/shard_map/ppermute | solution.py:17
  15.7 17.7 %collective-permute-start.16 = (bf16[8,256,128]{2,1,0:T(8,128)(2,1)S(1)}, bf16[8,256,128]{2,1,0:T(8,128)(2,1)}, u32[]{:S(2)}, u32[]{:S(2)}) collective-permute-start(bf16[8,256,128]{2,1,0:T(8,128)(2,1)S(1)} %bitcast.211), channel_id=1, source_target_pairs={{1,0},{2,1},{3,2},{4,3},{5,4},{6,5},{7,6},{8,7},{9,8},{10,9},{11,1... | collective-permute-start | bytes 1572872 | tf_op jit(solution)/shard_map/ppermute | solution.py:17
  25.7 16.1 %collective-permute-start.8 = (bf16[8,256,128]{2,1,0:T(8,128)(2,1)}, bf16[8,256,128]{2,1,0:T(8,128)(2,1)}, u32[]{:S(2)}, u32[]{:S(2)}) collective-permute-start(bf16[8,256,128]{2,1,0:T(8,128)(2,1)} %collective-permute-done.7), channel_id=1, source_target_pairs={{0,1},{1,2},{2,3},{3,4},{4,5},{5,6},{6,7},{7,8},{8,9},{9,10},{10,1... | collective-permute-start | bytes 1572872 | tf_op jit(solution)/shard_map/ppermute | solution.py:17
  27.7 16.1 %collective-permute-start.17 = (bf16[8,256,128]{2,1,0:T(8,128)(2,1)}, bf16[8,256,128]{2,1,0:T(8,128)(2,1)}, u32[]{:S(2)}, u32[]{:S(2)}) collective-permute-start(bf16[8,256,128]{2,1,0:T(8,128)(2,1)} %collective-permute-done.14), channel_id=1, source_target_pairs={{1,0},{2,1},{3,2},{4,3},{5,4},{6,5},{7,6},{8,7},{9,8},{10,9},{11,1... | collective-permute-start | bytes 1572872 | tf_op jit(solution)/shard_map/ppermute | solution.py:17
  33.4 16.1 %collective-permute-start.19 = (bf16[8,256,128]{2,1,0:T(8,128)(2,1)}, bf16[8,256,128]{2,1,0:T(8,128)(2,1)}, u32[]{:S(2)}, u32[]{:S(2)}) collective-permute-start(bf16[8,256,128]{2,1,0:T(8,128)(2,1)} %collective-permute-done.16), channel_id=1, source_target_pairs={{1,0},{2,1},{3,2},{4,3},{5,4},{6,5},{7,6},{8,7},{9,8},{10,9},{11,1... | collective-permute-start | bytes 1572872 | tf_op jit(solution)/shard_map/ppermute | solution.py:17
  36.2 17.3 %collective-permute-start.2 = (bf16[8,256,128]{2,1,0:T(8,128)(2,1)}, bf16[8,256,128]{2,1,0:T(8,128)(2,1)}, u32[]{:S(2)}, u32[]{:S(2)}) collective-permute-start(bf16[8,256,128]{2,1,0:T(8,128)(2,1)} %collective-permute-done.1), channel_id=1, source_target_pairs={{0,1},{1,2},{2,3},{3,4},{4,5},{5,6},{6,7},{7,8},{8,9},{9,10},{10,1... | collective-permute-start | bytes 1572872 | tf_op jit(solution)/shard_map/ppermute | solution.py:17
  41.8 16.4 %collective-permute-start.9 = (bf16[8,256,128]{2,1,0:T(8,128)(2,1)}, bf16[8,256,128]{2,1,0:T(8,128)(2,1)S(1)}, u32[]{:S(2)}, u32[]{:S(2)}) collective-permute-start(bf16[8,256,128]{2,1,0:T(8,128)(2,1)} %collective-permute-done.8), channel_id=1, source_target_pairs={{0,1},{1,2},{2,3},{3,4},{4,5},{5,6},{6,7},{7,8},{8,9},{9,10},{10,1... | collective-permute-start | bytes 1572872 | tf_op jit(solution)/shard_map/ppermute | solution.py:17
  43.8 16.4 %collective-permute-start.20 = (bf16[8,256,128]{2,1,0:T(8,128)(2,1)}, bf16[8,256,128]{2,1,0:T(8,128)(2,1)S(1)}, u32[]{:S(2)}, u32[]{:S(2)}) collective-permute-start(bf16[8,256,128]{2,1,0:T(8,128)(2,1)} %collective-permute-done.17), channel_id=1, source_target_pairs={{1,0},{2,1},{3,2},{4,3},{5,4},{6,5},{7,6},{8,7},{9,8},{10,9},{11,1... | collective-permute-start | bytes 1572872 | tf_op jit(solution)/shard_map/ppermute | solution.py:17
  49.5 16.4 %collective-permute-start.22 = (bf16[8,256,128]{2,1,0:T(8,128)(2,1)}, bf16[8,256,128]{2,1,0:T(8,128)(2,1)S(1)}, u32[]{:S(2)}, u32[]{:S(2)}) collective-permute-start(bf16[8,256,128]{2,1,0:T(8,128)(2,1)} %collective-permute-done.19), channel_id=1, source_target_pairs={{1,0},{2,1},{3,2},{4,3},{5,4},{6,5},{7,6},{8,7},{9,8},{10,9},{11,1... | collective-permute-start | bytes 1572872 | tf_op jit(solution)/shard_map/ppermute | solution.py:17
  53.5 16.8 %collective-permute-start.3 = (bf16[8,256,128]{2,1,0:T(8,128)(2,1)}, bf16[8,256,128]{2,1,0:T(8,128)(2,1)S(1)}, u32[]{:S(2)}, u32[]{:S(2)}) collective-permute-start(bf16[8,256,128]{2,1,0:T(8,128)(2,1)} %collective-permute-done.2), channel_id=1, source_target_pairs={{0,1},{1,2},{2,3},{3,4},{4,5},{5,6},{6,7},{7,8},{8,9},{9,10},{10,1... | collective-permute-start | bytes 1572872 | tf_op jit(solution)/shard_map/ppermute | solution.py:17
  74.5 16.0 %collective-permute-start.26 = (bf16[8,256,128]{2,1,0:T(8,128)(2,1)S(1)}, bf16[8,256,128]{2,1,0:T(8,128)(2,1)S(1)}, u32[]{:S(2)}, u32[]{:S(2)}) collective-permute-start(bf16[8,256,128]{2,1,0:T(8,128)(2,1)S(1)} %collective-permute-done.23), channel_id=1, source_target_pairs={{1,0},{2,1},{3,2},{4,3},{5,4},{6,5},{7,6},{8,7},{9,8},{10,9},{11,1... | collective-permute-start | bytes 1572872 | tf_op jit(solution)/shard_map/ppermute | solution.py:17
  80.3 16.0 %collective-permute-start.28 = (bf16[8,256,128]{2,1,0:T(8,128)(2,1)S(1)}, bf16[8,256,128]{2,1,0:T(8,128)(2,1)S(1)}, u32[]{:S(2)}, u32[]{:S(2)}) collective-permute-start(bf16[8,256,128]{2,1,0:T(8,128)(2,1)S(1)} %collective-permute-done.25), channel_id=1, source_target_pairs={{1,0},{2,1},{3,2},{4,3},{5,4},{6,5},{7,6},{8,7},{9,8},{10,9},{11,1... | collective-permute-start | bytes 1572872 | tf_op jit(solution)/shard_map/ppermute | solution.py:17
  99.6 16.0 %collective-permute-start.6 = (bf16[8,256,128]{2,1,0:T(8,128)(2,1)S(1)}, bf16[8,256,128]{2,1,0:T(8,128)(2,1)S(1)}, u32[]{:S(2)}, u32[]{:S(2)}) collective-permute-start(bf16[8,256,128]{2,1,0:T(8,128)(2,1)S(1)} %collective-permute-done.5), channel_id=1, source_target_pairs={{0,1},{1,2},{2,3},{3,4},{4,5},{5,6},{6,7},{7,8},{8,9},{9,10},{10,1... | collective-permute-start | bytes 1572872 | tf_op jit(solution)/shard_map/ppermute | solution.py:17
  104.4 45.9 %collective-permute-start.13 = (bf16[8,256,128]{2,1,0:T(8,128)(2,1)}, bf16[8,256,128]{2,1,0:T(8,128)(2,1)}, u32[]{:S(2)}, u32[]{:S(2)}) collective-permute-start(bf16[8,256,128]{2,1,0:T(8,128)(2,1)} %collective-permute-done.12), channel_id=1, source_target_pairs={{0,1},{1,2},{2,3},{3,4},{4,5},{5,6},{6,7},{7,8},{8,9},{9,10},{10,1... | collective-permute-start | bytes 1572872 | tf_op jit(solution)/shard_map/ppermute | solution.py:17
  106.3 119.3 %collective-permute-start.32 = (bf16[8,256,128]{2,1,0:T(8,128)(2,1)}, bf16[8,256,128]{2,1,0:T(8,128)(2,1)}, u32[]{:S(2)}, u32[]{:S(2)}) collective-permute-start(bf16[8,256,128]{2,1,0:T(8,128)(2,1)} %collective-permute-done.29), channel_id=1, source_target_pairs={{1,0},{2,1},{3,2},{4,3},{5,4},{6,5},{7,6},{8,7},{9,8},{10,9},{11,1... | collective-permute-start | bytes 1572872 | tf_op jit(solution)/shard_map/ppermute | solution.py:17
  112.1 120.7 %collective-permute-start.34 = (bf16[8,256,128]{2,1,0:T(8,128)(2,1)}, bf16[8,256,128]{2,1,0:T(8,128)(2,1)}, u32[]{:S(2)}, u32[]{:S(2)}) collective-permute-start(bf16[8,256,128]{2,1,0:T(8,128)(2,1)} %collective-permute-done.31), channel_id=1, source_target_pairs={{1,0},{2,1},{3,2},{4,3},{5,4},{6,5},{7,6},{8,7},{9,8},{10,9},{11,1... | collective-permute-start | bytes 1572872 | tf_op jit(solution)/shard_map/ppermute | solution.py:17
  120.3 38.1 %collective-permute-start.15 = (f32[8,512]{1,0:T(8,128)}, f32[8,512]{1,0:T(8,128)}, u32[]{:S(2)}, u32[]{:S(2)}) collective-permute-start(f32[8,512]{1,0:T(8,128)} %pad_maximum_fusion), channel_id=1, source_target_pairs={{1,0},{2,1},{3,2},{4,3},{5,4},{6,5},{7,6},{8,7},{9,8},{10,9},{11,1... | collective-permute-start | bytes 49160 | tf_op jit(solution)/shard_map/ppermute | solution.py:17
  122.3 41.6 %collective-permute-start.18 = (f32[8,512]{1,0:T(8,128)}, f32[8,512]{1,0:T(8,128)}, u32[]{:S(2)}, u32[]{:S(2)}) collective-permute-start(f32[8,512]{1,0:T(8,128)} %pad_maximum_fusion), channel_id=1, source_target_pairs={{2,0},{3,1},{4,2},{5,3},{6,4},{7,5},{8,6},{9,7},{10,8},{11,9},{12,... | collective-permute-start | bytes 49160 | tf_op jit(solution)/shard_map/ppermute | solution.py:17
  150.4 35.3 %collective-permute-start.21 = (f32[8,512]{1,0:T(8,128)}, f32[8,512]{1,0:T(8,128)S(1)}, u32[]{:S(2)}, u32[]{:S(2)}) collective-permute-start(f32[8,512]{1,0:T(8,128)} %pad_maximum_fusion), channel_id=1, source_target_pairs={{3,0},{4,1},{5,2},{6,3},{7,4},{8,5},{9,6},{10,7},{11,8},{12,9},{13... | collective-permute-start | bytes 49160 | tf_op jit(solution)/shard_map/ppermute | solution.py:17
  158.4 29.4 %collective-permute-start.24 = (f32[8,512]{1,0:T(8,128)}, f32[8,512]{1,0:T(8,128)S(1)}, u32[]{:S(2)}, u32[]{:S(2)}) collective-permute-start(f32[8,512]{1,0:T(8,128)} %pad_maximum_fusion), channel_id=1, source_target_pairs={{4,0},{5,1},{6,2},{7,3},{8,4},{9,5},{10,6},{11,7},{12,8},{13,9},{1... | collective-permute-start | bytes 49160 | tf_op jit(solution)/shard_map/ppermute | solution.py:17
  163.9 26.2 %collective-permute-start.27 = (f32[8,512]{1,0:T(8,128)}, f32[8,512]{1,0:T(8,128)S(1)}, u32[]{:S(2)}, u32[]{:S(2)}) collective-permute-start(f32[8,512]{1,0:T(8,128)} %pad_maximum_fusion), channel_id=1, source_target_pairs={{5,0},{6,1},{7,2},{8,3},{9,4},{10,5},{11,6},{12,7},{13,8},{14,9},{... | collective-permute-start | bytes 49160 | tf_op jit(solution)/shard_map/ppermute | solution.py:17
  187.8 33.8 %collective-permute-start.33 = (f32[8,512]{1,0:T(8,128)}, f32[8,512]{1,0:T(8,128)S(1)}, u32[]{:S(2)}, u32[]{:S(2)}) collective-permute-start(f32[8,512]{1,0:T(8,128)} %pad_maximum_fusion), channel_id=1, source_target_pairs={{7,0},{8,1},{9,2},{10,3},{11,4},{12,5},{13,6},{14,7},{15,8},{16,9}... | collective-permute-start | bytes 49160 | tf_op jit(solution)/shard_map/ppermute | solution.py:17
  (77 other events, 629.5 us)
